TPU v7x, 256 devices: a whole 4x4x8 slice. The times are simulated.
256 devices in a mesh: gy: 8 (over y, x_hi), gx: 4 (over x_lo, core), wa: 8 (over z).
Axes of the slice: x: 4 (x_hi: 2, x_lo: 2; x = x_hi * 2 + x_lo), y: 4, z: 8, core: 2. Of those that a mesh axis runs over, the one named last changes fastest.
Arguments:
- tokens: bfloat16 [8, 64, 128, 3072], P('wa', 'gy', 'gx'), may hold values from -6 to 6
- mod_shift: float32 [8, 3072], P('wa'), may hold values from -3 to 3
- mod_scale: float32 [8, 3072], P('wa'), may hold values from -0.9 to 3.9
- qkv_weight: bfloat16 [3072, 4608], P(None, ('gx', 'wa')), may hold values from -0.14433757 to 0.14433757
- block_codes: int32 [8, 16, 9], P('gy', 'gx'), may hold values from 0 to 8, as said below
- block_counts: int32 [8, 16], P('gy', 'gx'), may hold values from 1 to 9, as said below
- valid_tokens: int32 [8, 16], replicated, may hold values from 1 to 64
Outputs:
- attended: bfloat16 [8, 64, 128, 1536], P('wa', 'gy', 'gx')
Inputs may be any that keep to these rules, and one draw needn't show every extreme that they name: `block_codes`: the 9 codes of a block's list are distinct, the first is 4 (the block itself), and the first block_counts entries name blocks inside the grid. `block_counts`: A count never exceeds the number of blocks of the 3 x 3 neighbourhood that lie inside the grid.
All inputs are finite; a program needn't handle non-finite values.
Results may differ from a plain program's by a relative error of at most 0.007.
Values may be sent and summed in bfloat16 or wider, within the bound.
No kernel may reach another device: no remote copies, remote signals or barrier semaphores. Data moves between devices by JAX's collectives and lax.ppermute only.
A program may use at most 128 MiB of HBM per device.

v0:
```python
import math

import jax
import jax.numpy as jnp
from jax import lax
from jax.sharding import PartitionSpec as P

D = 3072
HEADS = 12
HD = 128
BLK = 8
NBR = 9


def extended_2(array, sides, width):
    for axis, dim in sides:
        size, length = (lax.axis_size(axis), array.shape[dim])
        up = [(i, (i + 1) % size) for i in range(size - 1)]
        down = [(j, i) for i, j in up]
        last = lax.slice_in_dim(array, length - width, length, axis=dim)
        first = lax.slice_in_dim(array, 0, width, axis=dim)
        before = lax.ppermute(last, axis, up)
        after = lax.ppermute(first, axis, down)
        array = jnp.concatenate([before, array, after], axis=dim)
    return array


def normalize(rows, shift_row, scale_row):
    widened = rows.astype(jnp.float32)
    average = jnp.mean(widened, axis=-1, keepdims=True)
    centred = widened - average
    spread = jnp.mean(centred * centred, axis=-1, keepdims=True)
    return (centred * lax.rsqrt(spread + 1e-06) * (1.0 + scale_row) + shift_row).astype(
        jnp.bfloat16
    )


def to_blocks(field):
    height, breadth, channels = field.shape
    shaped = field.reshape(height // BLK, BLK, breadth // BLK, BLK, channels)
    return shaped.transpose(0, 2, 1, 3, 4).reshape(
        height // BLK, breadth // BLK, BLK * BLK, channels
    )


def from_blocks(blocks):
    block_rows, block_cols, cells, channels = blocks.shape
    shaped = blocks.reshape(block_rows, block_cols, BLK, BLK, channels)
    return shaped.transpose(0, 2, 1, 3, 4).reshape(block_rows * BLK, block_cols * BLK, channels)


def make_mask(counts, live_count):
    slot_ids = jnp.arange(NBR, dtype=jnp.int32)
    token_ids = jnp.arange(BLK * BLK, dtype=jnp.int32)
    used = slot_ids[:, None] < counts[..., None, None]
    return used & (token_ids < live_count[..., None])


def attend(queries, key_blocks, key_mask):
    number = queries.shape[0]
    query_heads = queries.reshape(number, BLK * BLK, HEADS, HD)
    key_value = key_blocks.reshape(number, NBR * BLK * BLK, 2, HEADS, HD)
    scores = jnp.einsum(
        "nqhd,nkhd->nhqk", query_heads, key_value[:, :, 0], preferred_element_type=jnp.float32
    ) * (1.0 / math.sqrt(HD))
    scores = jnp.where(key_mask[:, None, None, :], scores, -jnp.inf)
    highest = jnp.max(scores, axis=-1, keepdims=True)
    exponent = jnp.exp(scores - highest)
    probs = (exponent / jnp.sum(exponent, axis=-1, keepdims=True)).astype(jnp.bfloat16)
    blended = jnp.einsum(
        "nhqk,nkhd->nqhd", probs, key_value[:, :, 1], preferred_element_type=jnp.float32
    )
    return blended.astype(jnp.bfloat16).reshape(number, BLK * BLK, HEADS * HD)


def body(tokens, mod_shift, mod_scale, qkv_weight, block_codes, block_counts, valid_tokens):
    tile_rows = tokens.shape[1]
    tile_cols = tokens.shape[2]
    width = HEADS * HD
    flat_rows = normalize(tokens[0], mod_shift[0], mod_scale[0]).reshape(tile_rows * tile_cols, D)
    qkv = jnp.dot(
        flat_rows,
        lax.all_gather(qkv_weight, ("gx", "wa"), axis=1, tiled=True),
        preferred_element_type=jnp.float32,
    ).astype(jnp.bfloat16)
    qkv_grid = qkv.reshape(tile_rows, tile_cols, 3 * width)
    extended = extended_2(qkv_grid[:, :, width:], (("gy", 0), ("gx", 1)), BLK)
    block_rows = tile_rows // BLK
    block_cols = tile_cols // BLK
    queries = to_blocks(qkv_grid[:, :, :width])
    key_blocks = to_blocks(extended)
    row_ids = jnp.arange(block_rows, dtype=jnp.int32)[:, None, None]
    col_ids = jnp.arange(block_cols, dtype=jnp.int32)[None, :, None]
    row_step = block_codes // 3 - 1
    col_step = block_codes % 3 - 1
    picked = key_blocks[row_ids + 1 + row_step, col_ids + 1 + col_step]
    global_row = jnp.clip(
        lax.axis_index("gy") * block_rows + row_ids + row_step, 0, valid_tokens.shape[0] - 1
    )
    global_col = jnp.clip(
        lax.axis_index("gx") * block_cols + col_ids + col_step, 0, valid_tokens.shape[1] - 1
    )
    live_count = valid_tokens[global_row, global_col]
    key_mask = make_mask(block_counts, live_count)
    number = block_rows * block_cols
    result = attend(
        queries.reshape(number, BLK * BLK, width),
        picked.reshape(number, NBR, BLK * BLK, 2 * width),
        key_mask.reshape(number, NBR * BLK * BLK),
    )
    return from_blocks(result.reshape(block_rows, block_cols, BLK * BLK, width))[None]


def solution(mesh):
    return jax.shard_map(
        body,
        mesh=mesh,
        in_specs=(
            P("wa", "gy", "gx", None),
            P("wa", None),
            P("wa", None),
            P(None, ("gx", "wa")),
            P("gy", "gx", None),
            P("gy", "gx"),
            P(),
        ),
        out_specs=P("wa", "gy", "gx", None),
        check_vma=False,
    )
```

profile of v0, /device:TPU:25, one launch (start us, length us, event | category | flops | bytes accessed | tf_op | source)
XLA Modules:
  0.0 367.9 jit_solution(4767164489304758296)
XLA Ops:
  7.3 1.7 convert_reduce_fusion
  9.1 2.0 fusion.8
  12.0 162.4 %all-gather.2.cloned.1.call-done = bf16[3072,4608]{0,1:T(8,128)(2,1)} async-done(((bf16[3072,144]{0,1:T(8,128)(2,1)}), bf16[3072,4608]{0,1:T(8,128)(2,1)}) %all-gather.2.cloned.1.call-update) | async-done | bytes 28311568 | tf_op jit(solution)/shard_map/all_gather | solution.py:83
  174.4 13.0 %convolution_convert_fusion = bf16[256,4608]{1,0:T(8,128)(2,1)S(1)} fusion(bf16[256,3072]{1,0:T(8,128)(2,1)S(1)} %fusion.12, bf16[3072,4608]{0,1:T(8,128)(2,1)} %all-gather.2.cloned.1.call-done), kind=kOutput, calls=%fused_computation.12 | convolution fusion | flops 7248936960 | bytes 32243712 | tf_op jit(solution)/shard_map/dot_general | solution.py:81
  187.6 1.2 copy-done.4
  188.8 4.7 %collective-permute-start.1 = (bf16[8,32,3072]{2,1,0:T(8,128)(2,1)S(1)}, bf16[8,32,3072]{2,1,0:T(8,128)(2,1)S(1)}, u32[]{:S(2)}, u32[]{:S(2)}) collective-permute-start(bf16[8,32,3072]{2,1,0:T(8,128)(2,1)S(1)} %slice.31), channel_id=1, source_target_pairs={{32,0},{64,32},{96,64},{128,96},{160,128},{192,160},{224,192},{33,... | collective-permute-start | bytes 4718600 | tf_op jit(solution)/shard_map/ppermute | solution.py:23
  193.5 2.2 collective-permute-start
  195.8 32.0 %collective-permute-done.1 = bf16[8,32,3072]{2,1,0:T(8,128)(2,1)S(1)} collective-permute-done((bf16[8,32,3072]{2,1,0:T(8,128)(2,1)S(1)}, bf16[8,32,3072]{2,1,0:T(8,128)(2,1)S(1)}, u32[]{:S(2)}, u32[]{:S(2)}) %collective-permute-start.1) | collective-permute-done | bytes 1572896 | tf_op jit(solution)/shard_map/ppermute | solution.py:23
  227.9 34.1 %collective-permute-done = bf16[8,32,3072]{2,1,0:T(8,128)(2,1)} collective-permute-done((bf16[8,32,3072]{2,1,0:T(8,128)(2,1)S(1)}, bf16[8,32,3072]{2,1,0:T(8,128)(2,1)}, u32[]{:S(2)}, u32[]{:S(2)}) %collective-permute-start) | collective-permute-done | bytes 1572896 | tf_op jit(solution)/shard_map/ppermute | solution.py:22
  261.9 2.8 pad_maximum_fusion.3
  264.7 3.5 collective-permute-start.2
  268.2 2.1 collective-permute-start.3
  272.0 1.2 slice_bitcast_fusion
  274.1 2.4 reshape_reshape_reshape.6
  276.5 5.2 %collective-permute-done.2 = bf16[24,8,3072]{2,1,0:T(8,128)(2,1)} collective-permute-done((bf16[24,8,3072]{2,1,0:T(8,128)(2,1)}, bf16[24,8,3072]{2,1,0:T(8,128)(2,1)}, u32[]{:S(2)}, u32[]{:S(2)}) %collective-permute-start.2) | collective-permute-done | bytes 1179680 | tf_op jit(solution)/shard_map/ppermute | solution.py:22
  281.7 4.4 %collective-permute-done.3 = bf16[24,8,3072]{2,1,0:T(8,128)(2,1)} collective-permute-done((bf16[24,8,3072]{2,1,0:T(8,128)(2,1)}, bf16[24,8,3072]{2,1,0:T(8,128)(2,1)}, u32[]{:S(2)}, u32[]{:S(2)}) %collective-permute-start.3) | collective-permute-done | bytes 1179680 | tf_op jit(solution)/shard_map/ppermute | solution.py:23
  286.1 3.3 pad_maximum_fusion
  289.4 3.7 %copy.33 = bf16[3,6,8,8,3072]{4,3,2,1,0:T(8,128)(2,1)} copy(bf16[3,6,8,8,3072]{4,3,1,2,0:T(8,128)(2,1)S(1)} %bitcast.68) | data formatting | bytes 14155776 | tf_op jit(solution)/shard_map/transpose | solution.py:41
  293.1 10.6 %gather_fusion = bf16[36,64,3072]{2,1,0:T(8,128)(2,1)} fusion(bf16[3,6,64,3072]{3,2,1,0:T(8,128)(2,1)} %bitcast.67, s32[36]{0:T(128)S(1)} %reshape.132), kind=kCustom, calls=%fused_computation | custom fusion | bytes 28311840 | tf_op jit(solution)/shard_map/gather | solution.py:96
  303.7 25.4 %reshape_reshape.3 = bf16[4,576,2,12,128]{4,3,2,1,0:T(8,128)(2,1)} reshape(bf16[36,64,3072]{2,1,0:T(8,128)(2,1)} %gather_fusion) | data formatting | bytes 28311552 | tf_op jit(solution)/shard_map/reshape;reshape | solution.py:62
  329.1 12.5 %fusion.30 = (bf16[4,576,1,12,128]{4,3,2,1,0:T(8,128)(2,1)S(1)}, bf16[4,576,1,12,128]{4,3,2,1,0:T(8,128)(2,1)}) fusion(bf16[4,576,2,12,128]{4,3,2,1,0:T(8,128)(2,1)} %reshape_reshape.3), kind=kLoop, calls=%fused_computation.69 | loop fusion | bytes 28311552 | tf_op jit(solution)/shard_map/slice | solution.py:64
  341.6 3.4 fusion.2
  345.0 4.4 %fusion.31 = (f32[4,12,64]{2,1,0:T(8,128)S(1)}, f32[4,12,64,576]{3,2,1,0:T(8,128)}) fusion(f32[4,12,64,576]{3,2,1,0:T(8,128)S(1)} %fusion.2, pred[4,576]{1,0:T(4,128)(4,1)S(1)} %compare_and_fusion), kind=kOutput, calls=%fused_computation.70 | output fusion | flops 10617407 | bytes 14170368 | tf_op jit(solution)/shard_map/sub | solution.py:68
  349.4 9.6 %fusion.14 = bf16[4,64,12,128]{3,1,2,0:T(8,128)(2,1)S(1)} fusion(bf16[4,576,1,12,128]{4,3,2,1,0:T(8,128)(2,1)} %get-tuple-element.6, f32[4,12,64,576]{3,2,1,0:T(8,128)} %get-tuple-element.14, f32[4,12,64]{2,1,0:T(8,128)S(1)} %get-tuple-element.13), kind=kOutput, calls=%fused_computation.27 | convolution fusion | flops 456916992 | bytes 14954496 | tf_op jit(solution)/shard_map/nhqk,nkhd->nqhd/dot_general | solution.py:70
  (48 shorter events, 6.6 us)
Async XLA Ops:
  6.5 263.9 %copy-start = (s32[8,16]{1,0:T(8,128)S(1)}, s32[8,16]{1,0:T(8,128)}, u32[]{:S(2)}) copy-start(s32[8,16]{1,0:T(8,128)} %param.13) | copy-start | bytes 1540
  6.5 4.6 %copy-start.2 = (bf16[1,8,32,3072]{3,2,1,0:T(8,128)(2,1)S(1)}, bf16[1,8,32,3072]{3,2,1,0:T(8,128)(2,1)}, u32[]{:S(2)}) copy-start(bf16[1,8,32,3072]{3,2,1,0:T(8,128)(2,1)} %param.7) | copy-start | bytes 4718596
  6.5 4.6 %copy-start.6 = (f32[1,3072]{1,0:T(1,128)S(1)}, f32[1,3072]{1,0:T(1,128)}, u32[]{:S(2)}) copy-start(f32[1,3072]{1,0:T(1,128)} %param.9) | copy-start | bytes 36868
  6.5 4.6 %copy-start.5 = (f32[1,3072]{1,0:T(1,128)S(1)}, f32[1,3072]{1,0:T(1,128)}, u32[]{:S(2)}) copy-start(f32[1,3072]{1,0:T(1,128)} %param.8) | copy-start | bytes 36868
  6.5 167.8 %all-gather.2.cloned.1.call-start = ((), (), s32[]{:S(2)}) async-start(), calls=%async_computation | async-start | bytes 29196288 | tf_op jit(solution)/shard_map/all_gather | solution.py:83
  12.0 183.8 %copy-start.7 = (s32[1,4,9]{2,1,0:T(4,128)S(1)}, s32[1,4,9]{2,1,0:T(4,128)}, u32[]{:S(2)}) copy-start(s32[1,4,9]{2,1,0:T(4,128)} %param.11) | copy-start | bytes 436
  187.4 1.4 copy-start.4
  188.8 39.1 %collective-permute-start.1 = (bf16[8,32,3072]{2,1,0:T(8,128)(2,1)S(1)}, bf16[8,32,3072]{2,1,0:T(8,128)(2,1)S(1)}, u32[]{:S(2)}, u32[]{:S(2)}) collective-permute-start(bf16[8,32,3072]{2,1,0:T(8,128)(2,1)S(1)} %slice.31), channel_id=1, source_target_pairs={{32,0},{64,32},{96,64},{128,96},{160,128},{192,160},{224,192},{33,... | collective-permute-start | bytes 4718600 | tf_op jit(solution)/shard_map/ppermute | solution.py:23
  193.5 68.4 %collective-permute-start = (bf16[8,32,3072]{2,1,0:T(8,128)(2,1)S(1)}, bf16[8,32,3072]{2,1,0:T(8,128)(2,1)}, u32[]{:S(2)}, u32[]{:S(2)}) collective-permute-start(bf16[8,32,3072]{2,1,0:T(8,128)(2,1)S(1)} %slice.31), channel_id=1, source_target_pairs={{0,32},{32,64},{64,96},{96,128},{128,160},{160,192},{192,224},{1,3... | collective-permute-start | bytes 4718600 | tf_op jit(solution)/shard_map/ppermute | solution.py:22
  195.8 75.7 %copy-start.8 = (s32[1,4]{1,0:T(1,128)S(1)}, s32[1,4]{1,0:T(1,128)}, u32[]{:S(2)}) copy-start(s32[1,4]{1,0:T(1,128)} %param.12) | copy-start | bytes 52
  264.7 16.9 %collective-permute-start.2 = (bf16[24,8,3072]{2,1,0:T(8,128)(2,1)}, bf16[24,8,3072]{2,1,0:T(8,128)(2,1)}, u32[]{:S(2)}, u32[]{:S(2)}) collective-permute-start(bf16[24,8,3072]{2,1,0:T(8,128)(2,1)} %get-tuple-element.7), channel_id=1, source_target_pairs={{0,8},{8,16},{16,24},{1,9},{9,17},{17,25},{2,10},{10,18},{18,26},{... | collective-permute-start | bytes 3538952 | tf_op jit(solution)/shard_map/ppermute | solution.py:22
  268.2 17.8 %collective-permute-start.3 = (bf16[24,8,3072]{2,1,0:T(8,128)(2,1)}, bf16[24,8,3072]{2,1,0:T(8,128)(2,1)}, u32[]{:S(2)}, u32[]{:S(2)}) collective-permute-start(bf16[24,8,3072]{2,1,0:T(8,128)(2,1)} %get-tuple-element.8), channel_id=1, source_target_pairs={{8,0},{16,8},{24,16},{9,1},{17,9},{25,17},{10,2},{18,10},{26,18},{... | collective-permute-start | bytes 3538952 | tf_op jit(solution)/shard_map/ppermute | solution.py:23
  329.1 12.5 %copy-start.3 = (bf16[4,64,12,128]{3,2,1,0:T(8,128)(2,1)S(1)}, bf16[4,64,12,128]{3,2,1,0:T(8,128)(2,1)}, u32[]{:S(2)}) copy-start(bf16[4,64,12,128]{3,2,1,0:T(8,128)(2,1)} %reshape_reshape_reshape.6) | copy-start | bytes 2359300
  349.4 11.6 %copy-start.1 = (s32[8,16]{1,0:T(8,128)S(1)}, s32[8,16]{1,0:T(8,128)}, u32[]{:S(2)}) copy-start(s32[8,16]{1,0:T(8,128)} %param.13) | copy-start | bytes 1540
Sparse Core Ops, SparseCore 0:
  9.2 165.1 all-gather.1
where the time goes:
time: 369 us; the launch traced here: 368 us
  waiting for transfers between devices  239 us (65%)
  local copies, waits for them, and re-layouts  61.9 us (17%)
  matrix products  26 us (7%)
  other arithmetic  15.2 us (4%)
  between operations  13.6 us (4%)
  starting transfers between devices  12.5 us (3%)
    all_gather x1, waiting for transfers between devices, body(): lax.all_gather(qkv_weight, ('gx', 'wa'), axis=1, tiled=True)  162 us
    ppermute x2, waiting for transfers between devices, extended_2(): before = lax.ppermute(last, axis, up)  39.2 us
    ppermute x2, waiting for transfers between devices, extended_2(): after = lax.ppermute(first, axis, down)  36.4 us
    another operation x1, local copies, waits for them, and re-layouts, attend(): key_value = key_blocks.reshape(number, NBR * BLK * BLK, 2, HEADS, HD)  25.4 us
    dot_general x1, matrix products, body(): jnp.dot(flat_rows, lax.all_gather(qkv_weight, ('gx', 'wa'), axis=1, tiled...  13 us
    slice x1, local copies, waits for them, and re-layouts, attend(): key_value[:, :, 0]  12.5 us
    gather x1, local copies, waits for them, and re-layouts, body(): picked = key_blocks[row_ids + 1 + row_step, col_ids + 1 + col_step]  10.6 us
    dot_general x1, matrix products, attend(): jnp.einsum('nhqk,nkhd->nqhd', probs, key_value[:, :, 1], preferred_elemen...  9.58 us
  transfers between devices with their start and end apart: 5, of which 5 were waited for; matrix products, arithmetic and copies ran while one was open for 3% of the time, Pallas kernels for 0%

commit v1 on v0

--- a/solution.py
+++ b/solution.py
@@ -77,12 +77,13 @@
     tile_rows = tokens.shape[1]
     tile_cols = tokens.shape[2]
     width = HEADS * HD
+    weight_block = lax.all_gather(qkv_weight, "wa", axis=1, tiled=True)
     flat_rows = normalize(tokens[0], mod_shift[0], mod_scale[0]).reshape(tile_rows * tile_cols, D)
-    qkv = jnp.dot(
-        flat_rows,
-        lax.all_gather(qkv_weight, ("gx", "wa"), axis=1, tiled=True),
-        preferred_element_type=jnp.float32,
-    ).astype(jnp.bfloat16)
+    row_group = lax.all_gather(flat_rows, "gx", axis=0, tiled=True)
+    partial = jnp.dot(row_group, weight_block, preferred_element_type=jnp.float32).astype(
+        jnp.bfloat16
+    )
+    qkv = lax.all_to_all(partial, "gx", 0, 1, tiled=True)
     qkv_grid = qkv.reshape(tile_rows, tile_cols, 3 * width)
     extended = extended_2(qkv_grid[:, :, width:], (("gy", 0), ("gx", 1)), BLK)
     block_rows = tile_rows // BLK

time: 369 us -> 398 us (1.079)
  blocking collectives: 0 us -> 30.8 us
  waiting for transfers between devices: 239 us -> 229 us
  local copies, waits for them, and re-layouts: 61.9 us -> 66.2 us
    all_to_all x0 -> x1, blocking collectives: none -> 30.8 us  [body(): qkv = lax.all_to_all(partial, 'gx', 0, 1, tiled=True)]
    all_gather x1 -> x2, waiting for transfers between devices: 162 us -> 153 us  [the longest x1 83.9 us: body(): weight_block = lax.all_gather(qkv_weight, 'wa', axis=1, tiled=True)]
    reshape x0 -> x2, local copies, waits for them, and re-layouts: none -> 6.12 us  [the longest x1 3.74 us: to_blocks(): shaped = field.reshape(height // BLK, BLK, breadth // BLK, BLK, channels)]
  transfers between devices with their start and end apart: 5 -> 6, of which waited for: 5 -> 6; matrix products, arithmetic and copies ran while one was open for 3% -> 2% of each run, Pallas kernels for 0% -> 0%
where the time goes in v1:
time: 398 us; the launch traced here: 396 us
  waiting for transfers between devices  229 us (58%)
  local copies, waits for them, and re-layouts  66.2 us (17%)
  blocking collectives  30.8 us (8%)
  matrix products  25.5 us (6%)
  other arithmetic  18.4 us (5%)
  between operations  13.6 us (3%)
  starting transfers between devices  13.3 us (3%)
    all_gather x1, waiting for transfers between devices, body(): weight_block = lax.all_gather(qkv_weight, 'wa', axis=1, tiled=True)  83.9 us
    all_gather x1, waiting for transfers between devices, body(): row_group = lax.all_gather(flat_rows, 'gx', axis=0, tiled=True)  69 us
    ppermute x2, waiting for transfers between devices, extended_2(): before = lax.ppermute(last, axis, up)  39.3 us
    ppermute x2, waiting for transfers between devices, extended_2(): after = lax.ppermute(first, axis, down)  35.7 us
    all_to_all x1, blocking collectives, body(): qkv = lax.all_to_all(partial, 'gx', 0, 1, tiled=True)  30.8 us
    another operation x1, local copies, waits for them, and re-layouts, attend(): key_value = key_blocks.reshape(number, NBR * BLK * BLK, 2, HEADS, HD)  25.4 us
    slice x1, local copies, waits for them, and re-layouts, attend(): key_value[:, :, 0]  12.5 us
    dot_general x1, matrix products, body(): jnp.dot(row_group, weight_block, preferred_element_type=jnp.float32)  12.5 us
  transfers between devices with their start and end apart: 6, of which 6 were waited for; matrix products, arithmetic and copies ran while one was open for 2% of the time, Pallas kernels for 0%

profile of v1, /device:TPU:25, one launch (start us, length us, event | category | flops | bytes accessed | tf_op | source)
XLA Modules:
  0.0 396.4 jit_solution(5357344674858160736)
XLA Ops:
  11.1 3.3 fusion.12
  15.2 69.0 %all-gather.3.cloned.1.call-done = bf16[1024,3072]{1,0:T(8,128)(2,1)} async-done(((bf16[256,3072]{1,0:T(8,128)(2,1)}), bf16[1024,3072]{1,0:T(8,128)(2,1)}) %all-gather.3.cloned.1.call-update) | async-done | bytes 6291472 | tf_op jit(solution)/shard_map/all_gather | solution.py:82
  84.2 83.9 %all-gather.5.cloned.1.call-done = bf16[3072,1152]{0,1:T(8,128)(2,1)} async-done(((bf16[3072,144]{0,1:T(8,128)(2,1)}), bf16[3072,1152]{0,1:T(8,128)(2,1)}) %all-gather.5.cloned.1.call-update) | async-done | bytes 7077904 | tf_op jit(solution)/shard_map/all_gather | solution.py:80
  168.2 12.5 %convolution_convert_fusion = bf16[1024,1152]{1,0:T(8,128)(2,1)S(1)} fusion(bf16[1024,3072]{1,0:T(8,128)(2,1)} %all-gather.3.cloned.1.call-done, bf16[3072,1152]{0,1:T(8,128)(2,1)} %all-gather.5.cloned.1.call-done), kind=kOutput, calls=%fused_computation.16 | convolution fusion | flops 7248936960 | bytes 15728640 | tf_op jit(solution)/shard_map/dot_general | solution.py:83
  180.7 30.8 %all_to_all.16 = bf16[4,256,1152]{2,1,0:T(8,128)(2,1)S(1)} all-to-all(bf16[4,256,1152]{2,1,0:T(8,128)(2,1)S(1)} %bitcast.72), channel_id=1, replica_groups=mesh['gy'=8,'gx'=4,'wa'=8] {'gx'}, dimensions={0} | all-to-all | bytes 4718592 | tf_op jit(solution)/shard_map/all_to_all | solution.py:86
  213.3 2.4 reshape.129
  217.3 4.8 %collective-permute-start.1 = (bf16[8,32,3072]{2,1,0:T(8,128)(2,1)S(1)}, bf16[8,32,3072]{2,1,0:T(8,128)(2,1)S(1)}, u32[]{:S(2)}, u32[]{:S(2)}) collective-permute-start(bf16[8,32,3072]{2,1,0:T(8,128)(2,1)S(1)} %slice.31), channel_id=1, source_target_pairs={{32,0},{64,32},{96,64},{128,96},{160,128},{192,160},{224,192},{33,... | collective-permute-start | bytes 4718600 | tf_op jit(solution)/shard_map/ppermute | solution.py:23
  224.3 31.3 %collective-permute-done.1 = bf16[8,32,3072]{2,1,0:T(8,128)(2,1)S(1)} collective-permute-done((bf16[8,32,3072]{2,1,0:T(8,128)(2,1)S(1)}, bf16[8,32,3072]{2,1,0:T(8,128)(2,1)S(1)}, u32[]{:S(2)}, u32[]{:S(2)}) %collective-permute-start.1) | collective-permute-done | bytes 1572896 | tf_op jit(solution)/shard_map/ppermute | solution.py:23
  255.6 34.1 %collective-permute-done = bf16[8,32,3072]{2,1,0:T(8,128)(2,1)} collective-permute-done((bf16[8,32,3072]{2,1,0:T(8,128)(2,1)S(1)}, bf16[8,32,3072]{2,1,0:T(8,128)(2,1)}, u32[]{:S(2)}, u32[]{:S(2)}) %collective-permute-start) | collective-permute-done | bytes 1572896 | tf_op jit(solution)/shard_map/ppermute | solution.py:22
  289.7 2.8 pad_maximum_fusion.3
  292.4 4.3 %collective-permute-start.2 = (bf16[24,8,3072]{2,1,0:T(8,128)(2,1)}, bf16[24,8,3072]{2,1,0:T(8,128)(2,1)}, u32[]{:S(2)}, u32[]{:S(2)}) collective-permute-start(bf16[24,8,3072]{2,1,0:T(8,128)(2,1)} %get-tuple-element.7), channel_id=1, source_target_pairs={{0,8},{8,16},{16,24},{1,9},{9,17},{17,25},{2,10},{10,18},{18,26},{... | collective-permute-start | bytes 3538952 | tf_op jit(solution)/shard_map/ppermute | solution.py:22
  296.7 2.1 collective-permute-start.3
  300.4 2.1 copy_bitcast_fusion.10
  302.5 2.4 reshape_reshape_reshape.6
  304.9 5.2 %collective-permute-done.2 = bf16[24,8,3072]{2,1,0:T(8,128)(2,1)} collective-permute-done((bf16[24,8,3072]{2,1,0:T(8,128)(2,1)}, bf16[24,8,3072]{2,1,0:T(8,128)(2,1)}, u32[]{:S(2)}, u32[]{:S(2)}) %collective-permute-start.2) | collective-permute-done | bytes 1179680 | tf_op jit(solution)/shard_map/ppermute | solution.py:22
  310.1 4.4 %collective-permute-done.3 = bf16[24,8,3072]{2,1,0:T(8,128)(2,1)} collective-permute-done((bf16[24,8,3072]{2,1,0:T(8,128)(2,1)}, bf16[24,8,3072]{2,1,0:T(8,128)(2,1)}, u32[]{:S(2)}, u32[]{:S(2)}) %collective-permute-start.3) | collective-permute-done | bytes 1179680 | tf_op jit(solution)/shard_map/ppermute | solution.py:23
  314.5 3.3 pad_maximum_fusion
  317.8 3.7 copy.46
  321.6 10.5 %gather_fusion = bf16[36,64,3072]{2,1,0:T(8,128)(2,1)} fusion(bf16[3,6,64,3072]{3,2,1,0:T(8,128)(2,1)} %bitcast.69, s32[36]{0:T(128)S(1)} %reshape.136), kind=kCustom, calls=%fused_computation | custom fusion | bytes 28311840 | tf_op jit(solution)/shard_map/gather | solution.py:97
  332.1 25.4 %reshape_reshape.3 = bf16[4,576,2,12,128]{4,3,2,1,0:T(8,128)(2,1)} reshape(bf16[36,64,3072]{2,1,0:T(8,128)(2,1)} %gather_fusion) | data formatting | bytes 28311552 | tf_op jit(solution)/shard_map/reshape;reshape | solution.py:62
  357.5 12.5 %fusion.30 = (bf16[4,576,1,12,128]{4,3,2,1,0:T(8,128)(2,1)S(1)}, bf16[4,576,1,12,128]{4,3,2,1,0:T(8,128)(2,1)}) fusion(bf16[4,576,2,12,128]{4,3,2,1,0:T(8,128)(2,1)} %reshape_reshape.3), kind=kLoop, calls=%fused_computation.70 | loop fusion | bytes 28311552 | tf_op jit(solution)/shard_map/slice | solution.py:64
  370.0 3.4 fusion.2
  373.5 4.4 %fusion.31 = (f32[4,12,64]{2,1,0:T(8,128)S(1)}, f32[4,12,64,576]{3,2,1,0:T(8,128)}) fusion(f32[4,12,64,576]{3,2,1,0:T(8,128)S(1)} %fusion.2, pred[4,576]{1,0:T(4,128)(4,1)S(1)} %compare_and_fusion), kind=kOutput, calls=%fused_computation.71 | output fusion | flops 10617407 | bytes 14170368 | tf_op jit(solution)/shard_map/sub | solution.py:68
  377.9 9.6 %fusion.14 = bf16[4,64,12,128]{3,1,2,0:T(8,128)(2,1)S(1)} fusion(bf16[4,576,1,12,128]{4,3,2,1,0:T(8,128)(2,1)} %get-tuple-element.6, f32[4,12,64,576]{3,2,1,0:T(8,128)} %get-tuple-element.14, f32[4,12,64]{2,1,0:T(8,128)S(1)} %get-tuple-element.13), kind=kOutput, calls=%fused_computation.27 | convolution fusion | flops 456916992 | bytes 14954496 | tf_op jit(solution)/shard_map/nhqk,nkhd->nqhd/dot_general | solution.py:70
  (45 shorter events, 14.5 us)
Async XLA Ops:
  6.5 292.4 %copy-start = (s32[8,16]{1,0:T(8,128)S(1)}, s32[8,16]{1,0:T(8,128)}, u32[]{:S(2)}) copy-start(s32[8,16]{1,0:T(8,128)} %param.13) | copy-start | bytes 1540
  6.5 77.7 %all-gather.3.cloned.1.call-start = ((), (), s32[]{:S(2)}) async-start(), calls=%async_computation.1 | async-start | bytes 7864320 | tf_op jit(solution)/shard_map/all_gather | solution.py:82
  14.5 153.7 %all-gather.5.cloned.1.call-start = ((), (), s32[]{:S(2)}) async-start(), calls=%async_computation.2 | async-start | bytes 7962624 | tf_op jit(solution)/shard_map/all_gather | solution.py:80
  213.3 10.9 %copy-start.3 = (s32[1,4,9]{2,1,0:T(4,128)S(1)}, s32[1,4,9]{2,1,0:T(4,128)}, u32[]{:S(2)}) copy-start(s32[1,4,9]{2,1,0:T(4,128)} %param.11) | copy-start | bytes 436
  217.3 82.7 %copy-start.4 = (s32[1,4]{1,0:T(1,128)S(1)}, s32[1,4]{1,0:T(1,128)}, u32[]{:S(2)}) copy-start(s32[1,4]{1,0:T(1,128)} %param.12) | copy-start | bytes 52
  217.3 38.3 %collective-permute-start.1 = (bf16[8,32,3072]{2,1,0:T(8,128)(2,1)S(1)}, bf16[8,32,3072]{2,1,0:T(8,128)(2,1)S(1)}, u32[]{:S(2)}, u32[]{:S(2)}) collective-permute-start(bf16[8,32,3072]{2,1,0:T(8,128)(2,1)S(1)} %slice.31), channel_id=1, source_target_pairs={{32,0},{64,32},{96,64},{128,96},{160,128},{192,160},{224,192},{33,... | collective-permute-start | bytes 4718600 | tf_op jit(solution)/shard_map/ppermute | solution.py:23
  222.1 67.6 %collective-permute-start = (bf16[8,32,3072]{2,1,0:T(8,128)(2,1)S(1)}, bf16[8,32,3072]{2,1,0:T(8,128)(2,1)}, u32[]{:S(2)}, u32[]{:S(2)}) collective-permute-start(bf16[8,32,3072]{2,1,0:T(8,128)(2,1)S(1)} %slice.31), channel_id=1, source_target_pairs={{0,32},{32,64},{64,96},{96,128},{128,160},{160,192},{192,224},{1,3... | collective-permute-start | bytes 4718600 | tf_op jit(solution)/shard_map/ppermute | solution.py:22
  292.4 17.7 %collective-permute-start.2 = (bf16[24,8,3072]{2,1,0:T(8,128)(2,1)}, bf16[24,8,3072]{2,1,0:T(8,128)(2,1)}, u32[]{:S(2)}, u32[]{:S(2)}) collective-permute-start(bf16[24,8,3072]{2,1,0:T(8,128)(2,1)} %get-tuple-element.7), channel_id=1, source_target_pairs={{0,8},{8,16},{16,24},{1,9},{9,17},{17,25},{2,10},{10,18},{18,26},{... | collective-permute-start | bytes 3538952 | tf_op jit(solution)/shard_map/ppermute | solution.py:22
  296.7 17.8 %collective-permute-start.3 = (bf16[24,8,3072]{2,1,0:T(8,128)(2,1)}, bf16[24,8,3072]{2,1,0:T(8,128)(2,1)}, u32[]{:S(2)}, u32[]{:S(2)}) collective-permute-start(bf16[24,8,3072]{2,1,0:T(8,128)(2,1)} %get-tuple-element.8), channel_id=1, source_target_pairs={{8,0},{16,8},{24,16},{9,1},{17,9},{25,17},{10,2},{18,10},{26,18},{... | collective-permute-start | bytes 3538952 | tf_op jit(solution)/shard_map/ppermute | solution.py:23
  357.5 12.5 %copy-start.2 = (bf16[4,64,12,128]{3,2,1,0:T(8,128)(2,1)S(1)}, bf16[4,64,12,128]{3,2,1,0:T(8,128)(2,1)}, u32[]{:S(2)}) copy-start(bf16[4,64,12,128]{3,2,1,0:T(8,128)(2,1)} %reshape_reshape_reshape.6) | copy-start | bytes 2359300
  377.9 11.6 %copy-start.1 = (s32[8,16]{1,0:T(8,128)S(1)}, s32[8,16]{1,0:T(8,128)}, u32[]{:S(2)}) copy-start(s32[8,16]{1,0:T(8,128)} %param.13) | copy-start | bytes 1540
Sparse Core Ops, SparseCore 0:
  14.6 69.5 all-gather.2
  86.0 82.0 all-gather.4

commit v2 on v0

--- a/solution.py
+++ b/solution.py
@@ -1,8 +1,11 @@
+import functools
 import math
 
 import jax
 import jax.numpy as jnp
 from jax import lax
+from jax.experimental import pallas as pl
+from jax.experimental.pallas import tpu as pltpu
 from jax.sharding import PartitionSpec as P
 
 D = 3072
@@ -10,6 +13,7 @@
 HD = 128
 BLK = 8
 NBR = 9
+CELLS = BLK * BLK
 
 
 def extended_2(array, sides, width):
@@ -49,28 +53,85 @@
     return shaped.transpose(0, 2, 1, 3, 4).reshape(block_rows * BLK, block_cols * BLK, channels)
 
 
-def make_mask(counts, live_count):
-    slot_ids = jnp.arange(NBR, dtype=jnp.int32)
-    token_ids = jnp.arange(BLK * BLK, dtype=jnp.int32)
-    used = slot_ids[:, None] < counts[..., None, None]
-    return used & (token_ids < live_count[..., None])
+def attend_kernel(block_cols, codes_ref, counts_ref, live_ref, q_ref, kv_hbm, o_ref, kv_buf, sems):
+    j = pl.program_id(0)
+    n_blocks = pl.num_programs(0)
+    ext_cols = block_cols + 2
+
+    def copies(block, slot):
+        out = []
+        for l in range(NBR):
+            code = jnp.clip(codes_ref[block * NBR + l], 0, NBR - 1)
+            src = (block // block_cols + code // 3) * ext_cols + block % block_cols + code % 3
+            out.append(
+                pltpu.make_async_copy(
+                    kv_hbm.at[src], kv_buf.at[slot, pl.ds(l * CELLS, CELLS)], sems.at[slot, l]
+                )
+            )
+        return out
+
+    @pl.when(j == 0)
+    def _():
+        for c in copies(j, 0):
+            c.start()
+
+    slot = j % 2
+
+    @pl.when(j + 1 < n_blocks)
+    def _():
+        for c in copies(j + 1, 1 - slot):
+            c.start()
+
+    for c in copies(j, slot):
+        c.wait()
+
+    count = counts_ref[j]
+    key_ids = lax.broadcasted_iota(jnp.int32, (CELLS, NBR * CELLS), 1)
+    key_slot = key_ids // CELLS
+    key_token = key_ids % CELLS
+    limit = jnp.zeros((CELLS, NBR * CELLS), jnp.int32)
+    for l in range(NBR):
+        thr = jnp.where(l < count, live_ref[j * NBR + l], 0)
+        limit = jnp.where(key_slot == l, thr, limit)
+    live = key_token < limit
+    width = HEADS * HD
+    for h in range(HEADS):
+        q = q_ref[0, :, h * HD:(h + 1) * HD]
+        k = kv_buf[slot, :, h * HD:(h + 1) * HD]
+        v = kv_buf[slot, :, width + h * HD:width + (h + 1) * HD]
+        s = lax.dot_general(
+            q, k, (((1,), (1,)), ((), ())), preferred_element_type=jnp.float32
+        ) * (1.0 / math.sqrt(HD))
+        s = jnp.where(live, s, -jnp.inf)
+        m = jnp.max(s, axis=-1, keepdims=True)
+        e = jnp.exp(s - m)
+        p = (e / jnp.sum(e, axis=-1, keepdims=True)).astype(jnp.bfloat16)
+        o = jnp.dot(p, v, preferred_element_type=jnp.float32)
+        o_ref[0, :, h * HD:(h + 1) * HD] = o.astype(o_ref.dtype)
 
 
-def attend(queries, key_blocks, key_mask):
-    number = queries.shape[0]
-    query_heads = queries.reshape(number, BLK * BLK, HEADS, HD)
-    key_value = key_blocks.reshape(number, NBR * BLK * BLK, 2, HEADS, HD)
-    scores = jnp.einsum(
-        "nqhd,nkhd->nhqk", query_heads, key_value[:, :, 0], preferred_element_type=jnp.float32
-    ) * (1.0 / math.sqrt(HD))
-    scores = jnp.where(key_mask[:, None, None, :], scores, -jnp.inf)
-    highest = jnp.max(scores, axis=-1, keepdims=True)
-    exponent = jnp.exp(scores - highest)
-    probs = (exponent / jnp.sum(exponent, axis=-1, keepdims=True)).astype(jnp.bfloat16)
-    blended = jnp.einsum(
-        "nhqk,nkhd->nqhd", probs, key_value[:, :, 1], preferred_element_type=jnp.float32
+def local_attention(q_blocks, kv_blocks, codes, counts, live_count, block_cols):
+    n_blocks = q_blocks.shape[0]
+    width = q_blocks.shape[-1]
+    grid_spec = pltpu.PrefetchScalarGridSpec(
+        num_scalar_prefetch=3,
+        grid=(n_blocks,),
+        in_specs=[
+            pl.BlockSpec((1, CELLS, width), lambda j, *_: (j, 0, 0)),
+            pl.BlockSpec(memory_space=pl.ANY),
+        ],
+        out_specs=pl.BlockSpec((1, CELLS, width), lambda j, *_: (j, 0, 0)),
+        scratch_shapes=[
+            pltpu.VMEM((2, NBR * CELLS, 2 * width), jnp.bfloat16),
+            pltpu.SemaphoreType.DMA((2, NBR)),
+        ],
     )
-    return blended.astype(jnp.bfloat16).reshape(number, BLK * BLK, HEADS * HD)
+    return pl.pallas_call(
+        functools.partial(attend_kernel, block_cols),
+        grid_spec=grid_spec,
+        out_shape=jax.ShapeDtypeStruct(q_blocks.shape, jnp.bfloat16),
+        compiler_params=pltpu.CompilerParams(dimension_semantics=("arbitrary",)),
+    )(codes.reshape(-1), counts.reshape(-1), live_count.reshape(-1), q_blocks, kv_blocks)
 
 
 def body(tokens, mod_shift, mod_scale, qkv_weight, block_codes, block_counts, valid_tokens):
@@ -93,7 +154,6 @@
     col_ids = jnp.arange(block_cols, dtype=jnp.int32)[None, :, None]
     row_step = block_codes // 3 - 1
     col_step = block_codes % 3 - 1
-    picked = key_blocks[row_ids + 1 + row_step, col_ids + 1 + col_step]
     global_row = jnp.clip(
         lax.axis_index("gy") * block_rows + row_ids + row_step, 0, valid_tokens.shape[0] - 1
     )
@@ -101,14 +161,16 @@
         lax.axis_index("gx") * block_cols + col_ids + col_step, 0, valid_tokens.shape[1] - 1
     )
     live_count = valid_tokens[global_row, global_col]
-    key_mask = make_mask(block_counts, live_count)
     number = block_rows * block_cols
-    result = attend(
-        queries.reshape(number, BLK * BLK, width),
-        picked.reshape(number, NBR, BLK * BLK, 2 * width),
-        key_mask.reshape(number, NBR * BLK * BLK),
+    result = local_attention(
+        queries.reshape(number, CELLS, width),
+        key_blocks.reshape(-1, CELLS, 2 * width),
+        block_codes.reshape(number, NBR),
+        block_counts.reshape(number),
+        live_count.reshape(number, NBR),
+        block_cols,
     )
-    return from_blocks(result.reshape(block_rows, block_cols, BLK * BLK, width))[None]
+    return from_blocks(result.reshape(block_rows, block_cols, CELLS, width))[None]
 
 
 def solution(mesh):

time: 369 us -> 324 us (0.88)
  local copies, waits for them, and re-layouts: 61.9 us -> 10.6 us
  Pallas kernels: 0 us -> 23 us
  matrix products: 26 us -> 13 us
  other arithmetic: 15.2 us -> 7.83 us
    another operation x4 -> x3, local copies, waits for them, and re-layouts: 29.3 us -> 4.93 us  [the longest x1 2.19 us: body(): queries.reshape(number, CELLS, width)]
    pallas_call x0 -> x1, Pallas kernels: none -> 23 us  [local_attention(): pl.pallas_call(functools.partial(attend_kernel, block_cols), grid_spec=gr...]
    dot_general x2 -> x0, matrix products: 13 us -> none  [the longest x1 9.58 us: attend(): jnp.einsum('nhqk,nkhd->nqhd', probs, key_value[:, :, 1], preferred_elemen...]
    slice x1 -> x0, local copies, waits for them, and re-layouts: 12.5 us -> none  [attend(): key_value[:, :, 0]]
    gather x1 -> x0, local copies, waits for them, and re-layouts: 10.6 us -> none  [body(): picked = key_blocks[row_ids + 1 + row_step, col_ids + 1 + col_step]]
    sub x1 -> x0, other arithmetic: 4.44 us -> none  [attend(): exponent = jnp.exp(scores - highest)]
  transfers between devices with their start and end apart: 5 -> 5, of which waited for: 5 -> 5; matrix products, arithmetic and copies ran while one was open for 3% -> 2% of each run, Pallas kernels for 0% -> 0%
where the time goes in v2:
time: 324 us; the launch traced here: 321 us
  waiting for transfers between devices  240 us (74%)
  Pallas kernels  23 us (7%)
  between operations  13.5 us (4%)
  starting transfers between devices  13.4 us (4%)
  matrix products  13 us (4%)
  local copies, waits for them, and re-layouts  10.6 us (3%)
  other arithmetic  7.83 us (2%)
    all_gather x1, waiting for transfers between devices, body(): lax.all_gather(qkv_weight, ('gx', 'wa'), axis=1, tiled=True)  164 us
    ppermute x2, waiting for transfers between devices, extended_2(): before = lax.ppermute(last, axis, up)  39.3 us
    ppermute x2, waiting for transfers between devices, extended_2(): after = lax.ppermute(first, axis, down)  35.9 us
    pallas_call x1, Pallas kernels, local_attention(): pl.pallas_call(functools.partial(attend_kernel, block_cols), grid_spec=gr...  23 us
    dot_general x1, matrix products, body(): jnp.dot(flat_rows, lax.all_gather(qkv_weight, ('gx', 'wa'), axis=1, tiled...  13 us
    ppermute x2, starting transfers between devices, extended_2(): before = lax.ppermute(last, axis, up)  8.09 us
  transfers between devices with their start and end apart: 5, of which 5 were waited for; matrix products, arithmetic and copies ran while one was open for 2% of the time, Pallas kernels for 0%

profile of v2, /device:TPU:25, one launch (start us, length us, event | category | flops | bytes accessed | tf_op | source)
XLA Modules:
  0.0 321.0 jit_solution(11840450618385500165)
XLA Ops:
  6.6 0.7 all-gather.2.cloned.1.call-update
  7.3 1.7 convert_reduce_fusion
  9.1 0.6 fusion.1
  9.7 0.8 fusion.5
  10.5 163.8 %all-gather.2.cloned.1.call-done = bf16[3072,4608]{0,1:T(8,128)(2,1)} async-done(((bf16[3072,144]{0,1:T(8,128)(2,1)}), bf16[3072,4608]{0,1:T(8,128)(2,1)}) %all-gather.2.cloned.1.call-update) | async-done | bytes 28311568 | tf_op jit(solution)/shard_map/all_gather | solution.py:144
  174.4 13.0 %convolution_convert_fusion = bf16[256,4608]{1,0:T(8,128)(2,1)S(1)} fusion(bf16[256,3072]{1,0:T(8,128)(2,1)S(1)} %fusion.5, bf16[3072,4608]{0,1:T(8,128)(2,1)} %all-gather.2.cloned.1.call-done), kind=kOutput, calls=%fused_computation.2 | convolution fusion | flops 7248936960 | bytes 32243712 | tf_op jit(solution)/shard_map/dot_general | solution.py:142
  187.4 0.2 slice.21
  187.6 4.6 %collective-permute-start = (bf16[8,32,3072]{2,1,0:T(8,128)(2,1)S(1)}, bf16[8,32,3072]{2,1,0:T(8,128)(2,1)S(1)}, u32[]{:S(2)}, u32[]{:S(2)}) collective-permute-start(bf16[8,32,3072]{2,1,0:T(8,128)(2,1)S(1)} %slice.21), channel_id=1, source_target_pairs={{0,32},{32,64},{64,96},{96,128},{128,160},{160,192},{192,224},{1,3... | collective-permute-start | bytes 4718600 | tf_op jit(solution)/shard_map/ppermute | solution.py:26
  192.2 3.2 %collective-permute-start.1 = (bf16[8,32,3072]{2,1,0:T(8,128)(2,1)S(1)}, bf16[8,32,3072]{2,1,0:T(8,128)(2,1)S(1)}, u32[]{:S(2)}, u32[]{:S(2)}) collective-permute-start(bf16[8,32,3072]{2,1,0:T(8,128)(2,1)S(1)} %slice.21), channel_id=1, source_target_pairs={{32,0},{64,32},{96,64},{128,96},{160,128},{192,160},{224,192},{33,... | collective-permute-start | bytes 4718600 | tf_op jit(solution)/shard_map/ppermute | solution.py:27
  195.4 32.3 %collective-permute-done = bf16[8,32,3072]{2,1,0:T(8,128)(2,1)S(1)} collective-permute-done((bf16[8,32,3072]{2,1,0:T(8,128)(2,1)S(1)}, bf16[8,32,3072]{2,1,0:T(8,128)(2,1)S(1)}, u32[]{:S(2)}, u32[]{:S(2)}) %collective-permute-start) | collective-permute-done | bytes 1572896 | tf_op jit(solution)/shard_map/ppermute | solution.py:26
  227.7 31.5 %collective-permute-done.1 = bf16[8,32,3072]{2,1,0:T(8,128)(2,1)S(1)} collective-permute-done((bf16[8,32,3072]{2,1,0:T(8,128)(2,1)S(1)}, bf16[8,32,3072]{2,1,0:T(8,128)(2,1)S(1)}, u32[]{:S(2)}, u32[]{:S(2)}) %collective-permute-start.1) | collective-permute-done | bytes 1572896 | tf_op jit(solution)/shard_map/ppermute | solution.py:27
  259.2 1.8 pad_maximum_fusion.3
  261.0 0.1 copy-done.2
  261.1 3.5 %collective-permute-start.2 = (bf16[24,8,3072]{2,1,0:T(8,128)(2,1)}, bf16[24,8,3072]{2,1,0:T(8,128)(2,1)}, u32[]{:S(2)}, u32[]{:S(2)}) collective-permute-start(bf16[24,8,3072]{2,1,0:T(8,128)(2,1)} %get-tuple-element.5), channel_id=1, source_target_pairs={{0,8},{8,16},{16,24},{1,9},{9,17},{17,25},{2,10},{10,18},{18,26},{... | collective-permute-start | bytes 3538952 | tf_op jit(solution)/shard_map/ppermute | solution.py:26
  264.6 2.0 collective-permute-start.3
  266.6 0.7 reshape_reshape.15.codes_ref
  267.5 1.4 gather_fusion
  268.9 2.2 copy_bitcast_fusion.1.q_ref
  271.0 7.0 %collective-permute-done.2 = bf16[24,8,3072]{2,1,0:T(8,128)(2,1)} collective-permute-done((bf16[24,8,3072]{2,1,0:T(8,128)(2,1)}, bf16[24,8,3072]{2,1,0:T(8,128)(2,1)}, u32[]{:S(2)}, u32[]{:S(2)}) %collective-permute-start.2) | collective-permute-done | bytes 1179680 | tf_op jit(solution)/shard_map/ppermute | solution.py:26
  278.0 4.4 %collective-permute-done.3 = bf16[24,8,3072]{2,1,0:T(8,128)(2,1)} collective-permute-done((bf16[24,8,3072]{2,1,0:T(8,128)(2,1)}, bf16[24,8,3072]{2,1,0:T(8,128)(2,1)}, u32[]{:S(2)}, u32[]{:S(2)}) %collective-permute-start.3) | collective-permute-done | bytes 1179680 | tf_op jit(solution)/shard_map/ppermute | solution.py:27
  282.4 2.9 pad_maximum_fusion
  285.3 3.7 %copy.10 = bf16[3,6,8,8,3072]{4,3,2,1,0:T(8,128)(2,1)} copy(bf16[3,6,8,8,3072]{4,3,1,2,0:T(8,128)(2,1)S(1)} %bitcast.48) | data formatting | bytes 14155776 | tf_op jit(solution)/shard_map/transpose | solution.py:45
  289.1 23.0 %shard_map.73 = bf16[4,64,1536]{2,1,0:T(8,128)(2,1)} custom-call(s32[36]{0:T(128)} %reshape_reshape.15.codes_ref, s32[4]{0:T(128)} %bitcast.54, s32[36]{0:T(128)} %gather_fusion, bf16[4,64,1536]{2,1,0:T(8,128)(2,1)} %copy_bitcast_fusion.1.q_ref, bf16[18,64,3072]{2,1,0:T(8,128)(2,1)} %bitcast.49), custom_call_target="tpu_custom_call" | custom-call | tf_op jit(solution)/shard_map/pallas_call | solution.py:129
  312.0 2.1 copy_bitcast_fusion
  (26 shorter events, 0.4 us)
Async XLA Ops:
  6.5 260.9 %copy-start = (s32[8,16]{1,0:T(8,128)S(1)}, s32[8,16]{1,0:T(8,128)}, u32[]{:S(2)}) copy-start(s32[8,16]{1,0:T(8,128)} %param.13) | copy-start | bytes 1540
  6.5 2.5 copy-start.1
  6.5 3.2 copy-start.6
  6.5 3.2 copy-start.5
  6.5 167.8 %all-gather.2.cloned.1.call-start = ((), (), s32[]{:S(2)}) async-start(), calls=%async_computation | async-start | bytes 29196288 | tf_op jit(solution)/shard_map/all_gather | solution.py:144
  187.4 73.6 %copy-start.4 = (bf16[256,4608]{1,0:T(8,128)(2,1)}, bf16[256,4608]{1,0:T(8,128)(2,1)S(1)}, u32[]{:S(2)}) copy-start(bf16[256,4608]{1,0:T(8,128)(2,1)S(1)} %convolution_convert_fusion) | copy-start | bytes 7077892
  187.6 79.0 %copy-start.7 = (s32[1,4,9]{2,1,0:T(4,128)S(1)}, s32[1,4,9]{2,1,0:T(4,128)}, u32[]{:S(2)}) copy-start(s32[1,4,9]{2,1,0:T(4,128)} %param.11) | copy-start | bytes 436
  187.6 40.1 %collective-permute-start = (bf16[8,32,3072]{2,1,0:T(8,128)(2,1)S(1)}, bf16[8,32,3072]{2,1,0:T(8,128)(2,1)S(1)}, u32[]{:S(2)}, u32[]{:S(2)}) collective-permute-start(bf16[8,32,3072]{2,1,0:T(8,128)(2,1)S(1)} %slice.21), channel_id=1, source_target_pairs={{0,32},{32,64},{64,96},{96,128},{128,160},{160,192},{192,224},{1,3... | collective-permute-start | bytes 4718600 | tf_op jit(solution)/shard_map/ppermute | solution.py:26
  192.2 67.0 %collective-permute-start.1 = (bf16[8,32,3072]{2,1,0:T(8,128)(2,1)S(1)}, bf16[8,32,3072]{2,1,0:T(8,128)(2,1)S(1)}, u32[]{:S(2)}, u32[]{:S(2)}) collective-permute-start(bf16[8,32,3072]{2,1,0:T(8,128)(2,1)S(1)} %slice.21), channel_id=1, source_target_pairs={{32,0},{64,32},{96,64},{128,96},{160,128},{192,160},{224,192},{33,... | collective-permute-start | bytes 4718600 | tf_op jit(solution)/shard_map/ppermute | solution.py:27
  259.2 1.9 copy-start.2
  261.1 17.0 %collective-permute-start.2 = (bf16[24,8,3072]{2,1,0:T(8,128)(2,1)}, bf16[24,8,3072]{2,1,0:T(8,128)(2,1)}, u32[]{:S(2)}, u32[]{:S(2)}) collective-permute-start(bf16[24,8,3072]{2,1,0:T(8,128)(2,1)} %get-tuple-element.5), channel_id=1, source_target_pairs={{0,8},{8,16},{16,24},{1,9},{9,17},{17,25},{2,10},{10,18},{18,26},{... | collective-permute-start | bytes 3538952 | tf_op jit(solution)/shard_map/ppermute | solution.py:26
  264.6 17.8 %collective-permute-start.3 = (bf16[24,8,3072]{2,1,0:T(8,128)(2,1)}, bf16[24,8,3072]{2,1,0:T(8,128)(2,1)}, u32[]{:S(2)}, u32[]{:S(2)}) collective-permute-start(bf16[24,8,3072]{2,1,0:T(8,128)(2,1)} %get-tuple-element.6), channel_id=1, source_target_pairs={{8,0},{16,8},{24,16},{9,1},{17,9},{25,17},{10,2},{18,10},{26,18},{... | collective-permute-start | bytes 3538952 | tf_op jit(solution)/shard_map/ppermute | solution.py:27
  268.9 13.6 %copy-start.3 = (bf16[8,32,3072]{2,1,0:T(8,128)(2,1)S(1)}, bf16[8,32,3072]{2,1,0:T(8,128)(2,1)}, u32[]{:S(2)}) copy-start(bf16[8,32,3072]{2,1,0:T(8,128)(2,1)} %copy-done.2) | copy-start | bytes 4718596
Sparse Core Ops, SparseCore 0:
  9.2 165.1 all-gather.1

commit v3 on v2

--- a/solution.py
+++ b/solution.py
@@ -138,14 +138,25 @@
     tile_rows = tokens.shape[1]
     tile_cols = tokens.shape[2]
     width = HEADS * HD
+    rows_axis = lax.axis_size("gy")
+    to_next = [(i, i + 1) for i in range(rows_axis - 1)]
+    to_prev = [(i + 1, i) for i in range(rows_axis - 1)]
+    above = lax.ppermute(tokens[0], "gy", to_next)
+    below = lax.ppermute(tokens[0], "gy", to_prev)
+    weight = lax.all_gather(qkv_weight, ("gx", "wa"), axis=1, tiled=True)
     flat_rows = normalize(tokens[0], mod_shift[0], mod_scale[0]).reshape(tile_rows * tile_cols, D)
-    qkv = jnp.dot(
-        flat_rows,
-        lax.all_gather(qkv_weight, ("gx", "wa"), axis=1, tiled=True),
-        preferred_element_type=jnp.float32,
-    ).astype(jnp.bfloat16)
+    qkv = jnp.dot(flat_rows, weight, preferred_element_type=jnp.float32).astype(jnp.bfloat16)
+    halo_rows = normalize(
+        jnp.concatenate([above, below], axis=0), mod_shift[0], mod_scale[0]
+    ).reshape(2 * tile_rows * tile_cols, D)
+    halo_kv = jnp.dot(
+        halo_rows, weight[:, width:], preferred_element_type=jnp.float32
+    ).astype(jnp.bfloat16).reshape(2 * tile_rows, tile_cols, 2 * width)
     qkv_grid = qkv.reshape(tile_rows, tile_cols, 3 * width)
-    extended = extended_2(qkv_grid[:, :, width:], (("gy", 0), ("gx", 1)), BLK)
+    extended = jnp.concatenate(
+        [halo_kv[:tile_rows], qkv_grid[:, :, width:], halo_kv[tile_rows:]], axis=0
+    )
+    extended = extended_2(extended, (("gx", 1),), BLK)
     block_rows = tile_rows // BLK
     block_cols = tile_cols // BLK
     queries = to_blocks(qkv_grid[:, :, :width])

time: 324 us -> 322 us (level)
  waiting for transfers between devices: 240 us -> 218 us
  matrix products: 13 us -> 27 us
  other arithmetic: 7.83 us -> 12.6 us
    ppermute x0 -> x2, waiting for transfers between devices: none -> 87.7 us  [the longest x1 49.7 us: body(): below = lax.ppermute(tokens[0], 'gy', to_prev)]
    all_gather x1, waiting for transfers between devices: 164 us -> 119 us  [body(): weight = lax.all_gather(qkv_weight, ('gx', 'wa'), axis=1, tiled=True)]
    ppermute x2 -> x1, waiting for transfers between devices: 39.3 us -> 6.95 us  [extended_2(): before = lax.ppermute(last, axis, up)]
    ppermute x2 -> x1, waiting for transfers between devices: 35.9 us -> 4.4 us  [extended_2(): after = lax.ppermute(first, axis, down)]
    dot_general x1 -> x2, matrix products: 13 us -> 27 us  [the longest x1 13.8 us: body(): jnp.dot(halo_rows, weight[:, width:], preferred_element_type=jnp.float32)]
    ppermute x0 -> x2, starting transfers between devices: none -> 7.69 us  [the longest x1 4.65 us: body(): above = lax.ppermute(tokens[0], 'gy', to_next)]
    ppermute x2 -> x1, starting transfers between devices: 8.09 us -> 3.56 us  [extended_2(): before = lax.ppermute(last, axis, up)]
  transfers between devices with their start and end apart: 5 -> 5, of which waited for: 5 -> 5; matrix products, arithmetic and copies ran while one was open for 2% -> 4% of each run, Pallas kernels for 0% -> 0%
where the time goes in v3:
time: 322 us; the launch traced here: 321 us
  waiting for transfers between devices  218 us (68%)
  matrix products  27 us (8%)
  Pallas kernels  23.4 us (7%)
  between operations  13.6 us (4%)
  starting transfers between devices  13.4 us (4%)
  local copies, waits for them, and re-layouts  12.9 us (4%)
  other arithmetic  12.6 us (4%)
    all_gather x1, waiting for transfers between devices, body(): weight = lax.all_gather(qkv_weight, ('gx', 'wa'), axis=1, tiled=True)  119 us
    ppermute x1, waiting for transfers between devices, body(): below = lax.ppermute(tokens[0], 'gy', to_prev)  49.7 us
    ppermute x1, waiting for transfers between devices, body(): above = lax.ppermute(tokens[0], 'gy', to_next)  38 us
    pallas_call x1, Pallas kernels, local_attention(): pl.pallas_call(functools.partial(attend_kernel, block_cols), grid_spec=gr...  23.4 us
    dot_general x1, matrix products, body(): jnp.dot(halo_rows, weight[:, width:], preferred_element_type=jnp.float32)  13.8 us
    dot_general x1, matrix products, body(): jnp.dot(flat_rows, weight, preferred_element_type=jnp.float32)  13.2 us
    ppermute x1, waiting for transfers between devices, extended_2(): before = lax.ppermute(last, axis, up)  6.95 us
  transfers between devices with their start and end apart: 5, of which 5 were waited for; matrix products, arithmetic and copies ran while one was open for 4% of the time, Pallas kernels for 0%

profile of v3, /device:TPU:25, one launch (start us, length us, event | category | flops | bytes accessed | tf_op | source)
XLA Modules:
  0.0 321.2 jit_solution(16957069343895259354)
XLA Ops:
  6.5 0.7 all-gather.2.cloned.1.call-update
  7.3 4.7 %collective-permute-start = (bf16[8,32,3072]{2,1,0:T(8,128)(2,1)}, bf16[8,32,3072]{2,1,0:T(8,128)(2,1)S(1)}, u32[]{:S(2)}, u32[]{:S(2)}) collective-permute-start(bf16[8,32,3072]{2,1,0:T(8,128)(2,1)} %bitcast.55), channel_id=1, source_target_pairs={{0,32},{32,64},{64,96},{96,128},{128,160},{160,192},{192,224},{1,3... | collective-permute-start | bytes 4718600 | tf_op jit(solution)/shard_map/ppermute | solution.py:144
  11.9 3.0 collective-permute-start.1
  15.0 1.7 convert_reduce_fusion
  16.8 2.0 fusion.10
  18.8 38.0 %collective-permute-done = bf16[8,32,3072]{2,1,0:T(8,128)(2,1)S(1)} collective-permute-done((bf16[8,32,3072]{2,1,0:T(8,128)(2,1)}, bf16[8,32,3072]{2,1,0:T(8,128)(2,1)S(1)}, u32[]{:S(2)}, u32[]{:S(2)}) %collective-permute-start) | collective-permute-done | bytes 1572896 | tf_op jit(solution)/shard_map/ppermute | solution.py:144
  56.8 49.7 %collective-permute-done.1 = bf16[8,32,3072]{2,1,0:T(8,128)(2,1)S(1)} collective-permute-done((bf16[8,32,3072]{2,1,0:T(8,128)(2,1)}, bf16[8,32,3072]{2,1,0:T(8,128)(2,1)S(1)}, u32[]{:S(2)}, u32[]{:S(2)}) %collective-permute-start.1) | collective-permute-done | bytes 1572896 | tf_op jit(solution)/shard_map/ppermute | solution.py:145
  107.1 1.0 multiply_reduce_fusion
  108.9 1.8 fusion.5
  110.7 118.6 %all-gather.2.cloned.1.call-done = bf16[3072,4608]{0,1:T(8,128)(2,1)} async-done(((bf16[3072,144]{0,1:T(8,128)(2,1)}), bf16[3072,4608]{0,1:T(8,128)(2,1)}) %all-gather.2.cloned.1.call-update) | async-done | bytes 28311568 | tf_op jit(solution)/shard_map/all_gather | solution.py:146
  229.3 13.8 %fusion.6 = bf16[512,3072]{1,0:T(8,128)(2,1)S(1)} fusion(bf16[512,3072]{1,0:T(8,128)(2,1)S(1)} %fusion.5, bf16[3072,4608]{0,1:T(8,128)(2,1)} %all-gather.2.cloned.1.call-done), kind=kOutput, calls=%fused_computation.11 | convolution fusion | flops 9665249280 | bytes 25165824 | tf_op jit(solution)/shard_map/dot_general | solution.py:152
  243.3 1.7 copy-done.2
  245.1 13.2 %convolution_convert_fusion = bf16[256,4608]{1,0:T(8,128)(2,1)S(1)} fusion(bf16[3072,4608]{0,1:T(8,128)(2,1)} %all-gather.2.cloned.1.call-done, bf16[256,3072]{1,0:T(8,128)(2,1)S(1)} %bitcast.57, f32[3072]{0:T(1024)S(1)} %bitcast.63, f32[3072]{0:T(1024)S(1)} %bitcast.61, f32[256]{0:T(256)S(1)} %rsqrt.23, f32[256]{0:T(256)S(1)} %div.24), kind=kOutput, calls=%fused_computation.4 | convolution fusion | flops 7253655552 | bytes 32270336 | tf_op jit(solution)/shard_map/dot_general | solution.py:148
  258.5 1.8 pad_maximum_fusion.3
  260.4 3.6 %collective-permute-start.2 = (bf16[24,8,3072]{2,1,0:T(8,128)(2,1)}, bf16[24,8,3072]{2,1,0:T(8,128)(2,1)}, u32[]{:S(2)}, u32[]{:S(2)}) collective-permute-start(bf16[24,8,3072]{2,1,0:T(8,128)(2,1)} %get-tuple-element.5), channel_id=1, source_target_pairs={{0,8},{8,16},{16,24},{1,9},{9,17},{17,25},{2,10},{10,18},{18,26},{... | collective-permute-start | bytes 3538952 | tf_op jit(solution)/shard_map/ppermute | solution.py:26
  264.0 2.1 collective-permute-start.3
  267.0 1.4 gather_fusion
  268.4 2.1 copy_bitcast_fusion.1.q_ref
  270.5 6.9 %collective-permute-done.2 = bf16[24,8,3072]{2,1,0:T(8,128)(2,1)} collective-permute-done((bf16[24,8,3072]{2,1,0:T(8,128)(2,1)}, bf16[24,8,3072]{2,1,0:T(8,128)(2,1)}, u32[]{:S(2)}, u32[]{:S(2)}) %collective-permute-start.2) | collective-permute-done | bytes 1179680 | tf_op jit(solution)/shard_map/ppermute | solution.py:26
  277.4 4.4 %collective-permute-done.3 = bf16[24,8,3072]{2,1,0:T(8,128)(2,1)} collective-permute-done((bf16[24,8,3072]{2,1,0:T(8,128)(2,1)}, bf16[24,8,3072]{2,1,0:T(8,128)(2,1)}, u32[]{:S(2)}, u32[]{:S(2)}) %collective-permute-start.3) | collective-permute-done | bytes 1179680 | tf_op jit(solution)/shard_map/ppermute | solution.py:27
  281.8 3.3 %pad_maximum_fusion = bf16[24,48,3072]{2,1,0:T(8,128)(2,1)S(1)} fusion(bf16[24,8,3072]{2,1,0:T(8,128)(2,1)} %collective-permute-done.3, bf16[8,32,3072]{2,1,0:T(8,128)(2,1)} %bitcast.54, bf16[8,32,3072]{2,1,0:T(8,128)(2,1)S(1)} %slice.43, bf16[8,32,3072]{2,1,0:T(8,128)(2,1)S(1)} %bitcast.52, bf16[24,8,3072]{2,1,0:T(8,128)(2,1)} %collective-permute-done.2), kind=kLoop, calls=%fused_computation.3 | loop fusion | flops 35389440 | bytes 14155776 | tf_op jit(solution)/shard_map/concatenate | solution.py:28
  285.1 3.7 %copy.10 = bf16[3,6,8,8,3072]{4,3,2,1,0:T(8,128)(2,1)} copy(bf16[3,6,8,8,3072]{4,3,1,2,0:T(8,128)(2,1)S(1)} %bitcast.49) | data formatting | bytes 14155776 | tf_op jit(solution)/shard_map/transpose | solution.py:45
  288.8 23.4 %shard_map.73 = bf16[4,64,1536]{2,1,0:T(8,128)(2,1)} custom-call(s32[36]{0:T(128)} %reshape_reshape.15.codes_ref, s32[4]{0:T(128)} %bitcast.64, s32[36]{0:T(128)} %gather_fusion, bf16[4,64,1536]{2,1,0:T(8,128)(2,1)} %copy_bitcast_fusion.1.q_ref, bf16[18,64,3072]{2,1,0:T(8,128)(2,1)} %bitcast.50), custom_call_target="tpu_custom_call" | custom-call | tf_op jit(solution)/shard_map/pallas_call | solution.py:129
  312.3 2.1 copy_bitcast_fusion
  (33 shorter events, 2.9 us)
Async XLA Ops:
  6.5 260.4 %copy-start = (s32[8,16]{1,0:T(8,128)S(1)}, s32[8,16]{1,0:T(8,128)}, u32[]{:S(2)}) copy-start(s32[8,16]{1,0:T(8,128)} %param.13) | copy-start | bytes 1540
  6.5 12.3 %copy-start.5 = (f32[1,3072]{1,0:T(1,128)S(1)}, f32[1,3072]{1,0:T(1,128)}, u32[]{:S(2)}) copy-start(f32[1,3072]{1,0:T(1,128)} %param.9) | copy-start | bytes 36868
  6.5 222.7 %all-gather.2.cloned.1.call-start = ((), (), s32[]{:S(2)}) async-start(), calls=%async_computation | async-start | bytes 29196288 | tf_op jit(solution)/shard_map/all_gather | solution.py:146
  7.3 49.6 %collective-permute-start = (bf16[8,32,3072]{2,1,0:T(8,128)(2,1)}, bf16[8,32,3072]{2,1,0:T(8,128)(2,1)S(1)}, u32[]{:S(2)}, u32[]{:S(2)}) collective-permute-start(bf16[8,32,3072]{2,1,0:T(8,128)(2,1)} %bitcast.55), channel_id=1, source_target_pairs={{0,32},{32,64},{64,96},{96,128},{128,160},{160,192},{192,224},{1,3... | collective-permute-start | bytes 4718600 | tf_op jit(solution)/shard_map/ppermute | solution.py:144
  11.9 94.6 %collective-permute-start.1 = (bf16[8,32,3072]{2,1,0:T(8,128)(2,1)}, bf16[8,32,3072]{2,1,0:T(8,128)(2,1)S(1)}, u32[]{:S(2)}, u32[]{:S(2)}) collective-permute-start(bf16[8,32,3072]{2,1,0:T(8,128)(2,1)} %bitcast.56), channel_id=1, source_target_pairs={{32,0},{64,32},{96,64},{128,96},{160,128},{192,160},{224,192},{33,... | collective-permute-start | bytes 4718600 | tf_op jit(solution)/shard_map/ppermute | solution.py:145
  108.2 0.7 copy-start.4
  243.1 2.0 copy-start.2
  243.3 15.1 %copy-start.1 = (bf16[256,3072]{1,0:T(8,128)(2,1)}, bf16[256,3072]{1,0:T(8,128)(2,1)S(1)}, u32[]{:S(2)}) copy-start(bf16[256,3072]{1,0:T(8,128)(2,1)S(1)} %get-tuple-element.8) | copy-start | bytes 4718596
  258.3 2.1 copy-start.3
  258.5 7.6 %copy-start.6 = (s32[1,4,9]{2,1,0:T(4,128)S(1)}, s32[1,4,9]{2,1,0:T(4,128)}, u32[]{:S(2)}) copy-start(s32[1,4,9]{2,1,0:T(4,128)} %param.11) | copy-start | bytes 436
  260.4 17.0 %collective-permute-start.2 = (bf16[24,8,3072]{2,1,0:T(8,128)(2,1)}, bf16[24,8,3072]{2,1,0:T(8,128)(2,1)}, u32[]{:S(2)}, u32[]{:S(2)}) collective-permute-start(bf16[24,8,3072]{2,1,0:T(8,128)(2,1)} %get-tuple-element.5), channel_id=1, source_target_pairs={{0,8},{8,16},{16,24},{1,9},{9,17},{17,25},{2,10},{10,18},{18,26},{... | collective-permute-start | bytes 3538952 | tf_op jit(solution)/shard_map/ppermute | solution.py:26
  264.0 17.8 %collective-permute-start.3 = (bf16[24,8,3072]{2,1,0:T(8,128)(2,1)}, bf16[24,8,3072]{2,1,0:T(8,128)(2,1)}, u32[]{:S(2)}, u32[]{:S(2)}) collective-permute-start(bf16[24,8,3072]{2,1,0:T(8,128)(2,1)} %get-tuple-element.6), channel_id=1, source_target_pairs={{8,0},{16,8},{24,16},{9,1},{17,9},{25,17},{10,2},{18,10},{26,18},{... | collective-permute-start | bytes 3538952 | tf_op jit(solution)/shard_map/ppermute | solution.py:27
Sparse Core Ops, SparseCore 0:
  9.1 220.0 all-gather.1

commit v4 on v2

--- a/solution.py
+++ b/solution.py
@@ -138,12 +138,29 @@
     tile_rows = tokens.shape[1]
     tile_cols = tokens.shape[2]
     width = HEADS * HD
-    flat_rows = normalize(tokens[0], mod_shift[0], mod_scale[0]).reshape(tile_rows * tile_cols, D)
-    qkv = jnp.dot(
-        flat_rows,
-        lax.all_gather(qkv_weight, ("gx", "wa"), axis=1, tiled=True),
+    group = lax.axis_size("gx")
+    me = lax.axis_index("gx")
+    tile = tokens[0]
+    received = [tile] + [
+        lax.ppermute(tile, "gx", [(i, (i + d) % group) for i in range(group)])
+        for d in range(1, group)
+    ]
+    weight_block = lax.all_gather(qkv_weight, "wa", axis=1, tiled=True)
+    strip = normalize(jnp.stack(received), mod_shift[0], mod_scale[0]).reshape(
+        group, tile_rows * tile_cols, D
+    )
+    partial = jnp.dot(
+        strip.reshape(group * tile_rows * tile_cols, D),
+        weight_block,
         preferred_element_type=jnp.float32,
-    ).astype(jnp.bfloat16)
+    ).astype(jnp.bfloat16).reshape(group, tile_rows * tile_cols, -1)
+    returned = [partial[0]] + [
+        lax.ppermute(partial[d], "gx", [(i, (i - d) % group) for i in range(group)])
+        for d in range(1, group)
+    ]
+    doubled = jnp.stack(returned + returned)
+    ordered = lax.dynamic_slice_in_dim(doubled, group - me, group, axis=0)
+    qkv = ordered.transpose(1, 0, 2).reshape(tile_rows * tile_cols, 3 * width)
     qkv_grid = qkv.reshape(tile_rows, tile_cols, 3 * width)
     extended = extended_2(qkv_grid[:, :, width:], (("gy", 0), ("gx", 1)), BLK)
     block_rows = tile_rows // BLK

time: 324 us -> 279 us (0.86)
  waiting for transfers between devices: 240 us -> 165 us
  other arithmetic: 7.83 us -> 20.7 us
  local copies, waits for them, and re-layouts: 10.6 us -> 19.4 us
  starting transfers between devices: 13.4 us -> 20.7 us
    all_gather x1, waiting for transfers between devices: 164 us -> 0.01 us  [body(): weight_block = lax.all_gather(qkv_weight, 'wa', axis=1, tiled=True)]
    ppermute x0 -> x6, waiting for transfers between devices: none -> 91.7 us  [the longest x3 68 us: body(): lax.ppermute(tile, 'gx', [(i, (i + d) % group) for i in range(group)])]
    ppermute x0 -> x6, starting transfers between devices: none -> 5.84 us  [the longest x3 3.49 us: body(): lax.ppermute(partial[d], 'gx', [(i, (i - d) % group) for i in range(group)])]
    convert_element_type x1, other arithmetic: 0.79 us -> 5.08 us  [normalize(): (centred * lax.rsqrt(spread + 1e-06) * (1.0 + scale_row) + shift_row).ast...]
    reduce_sum x1, other arithmetic: 0.55 us -> 3.85 us  [normalize(): spread = jnp.mean(centred * centred, axis=-1, keepdims=True)]
  transfers between devices with their start and end apart: 5 -> 11, of which waited for: 5 -> 9; matrix products, arithmetic and copies ran while one was open for 2% -> 7% of each run, Pallas kernels for 0% -> 0%
where the time goes in v4:
time: 279 us; the launch traced here: 275 us
  waiting for transfers between devices  165 us (59%)
  Pallas kernels  23 us (8%)
  starting transfers between devices  20.7 us (7%)
  other arithmetic  20.7 us (7%)
  local copies, waits for them, and re-layouts  19.4 us (7%)
  between operations  13.6 us (5%)
  matrix products  12.5 us (4%)
    ppermute x3, waiting for transfers between devices, body(): lax.ppermute(tile, 'gx', [(i, (i + d) % group) for i in range(group)])  68 us
    ppermute x2, waiting for transfers between devices, extended_2(): before = lax.ppermute(last, axis, up)  37.5 us
    ppermute x2, waiting for transfers between devices, extended_2(): after = lax.ppermute(first, axis, down)  35.5 us
    ppermute x3, waiting for transfers between devices, body(): lax.ppermute(partial[d], 'gx', [(i, (i - d) % group) for i in range(group)])  23.6 us
    pallas_call x1, Pallas kernels, local_attention(): pl.pallas_call(functools.partial(attend_kernel, block_cols), grid_spec=gr...  23 us
    dot_general x1, matrix products, body(): jnp.dot(strip.reshape(group * tile_rows * tile_cols, D), weight_block, pr...  12.5 us
    ppermute x2, starting transfers between devices, extended_2(): before = lax.ppermute(last, axis, up)  8.94 us
    ppermute x2, starting transfers between devices, extended_2(): after = lax.ppermute(first, axis, down)  5.89 us
  transfers between devices with their start and end apart: 11, of which 9 were waited for; matrix products, arithmetic and copies ran while one was open for 7% of the time, Pallas kernels for 0%

profile of v4, /device:TPU:25, one launch (start us, length us, event | category | flops | bytes accessed | tf_op | source)
XLA Modules:
  0.0 275.2 jit_solution(15880375068493146607)
XLA Ops:
  10.3 32.6 %collective-permute-done = bf16[8,32,3072]{2,1,0:T(8,128)(2,1)S(1)} collective-permute-done((bf16[8,32,3072]{2,1,0:T(8,128)(2,1)}, bf16[8,32,3072]{2,1,0:T(8,128)(2,1)S(1)}, u32[]{:S(2)}, u32[]{:S(2)}) %collective-permute-start) | collective-permute-done | bytes 1572896 | tf_op jit(solution)/shard_map/ppermute | solution.py:145
  43.0 34.7 %collective-permute-done.1 = bf16[8,32,3072]{2,1,0:T(8,128)(2,1)S(1)} collective-permute-done((bf16[8,32,3072]{2,1,0:T(8,128)(2,1)}, bf16[8,32,3072]{2,1,0:T(8,128)(2,1)S(1)}, u32[]{:S(2)}, u32[]{:S(2)}) %collective-permute-start.1) | collective-permute-done | bytes 1572896 | tf_op jit(solution)/shard_map/ppermute | solution.py:145
  78.8 2.8 %fusion.15 = f32[4,8,32]{2,1,0:T(8,128)S(1)} fusion(bf16[1,8,32,3072]{3,2,1,0:T(8,128)(2,1)S(1)} %bitcast.73, bf16[1,8,32,3072]{3,2,1,0:T(8,128)(2,1)S(1)} %bitcast.70, bf16[1,8,32,3072]{3,2,1,0:T(8,128)(2,1)S(1)} %bitcast.67, bf16[1,8,32,3072]{3,2,1,0:T(8,128)(2,1)} %param.7), kind=kLoop, calls=%fused_computation.48 | loop fusion | flops 15727616 | bytes 6295552 | tf_op jit(solution)/shard_map/reduce_sum | solution.py:34
  81.8 3.8 %multiply_reduce_fusion = f32[4,8,32]{2,1,0:T(8,128)S(1)} fusion(f32[4,8,32]{2,1,0:T(8,128)S(1)} %broadcast_multiply_fusion, bf16[1,8,32,3072]{3,2,1,0:T(8,128)(2,1)} %bitcast.74, bf16[1,8,32,3072]{3,2,1,0:T(8,128)(2,1)} %bitcast.71, bf16[1,8,32,3072]{3,2,1,0:T(8,128)(2,1)S(1)} %bitcast.68, bf16[1,8,32,3072]{3,2,1,0:T(8,128)(2,1)S(1)} %copy-done.1), kind=kLoop, calls=%fused_computation.6 | loop fusion | flops 22019072 | bytes 6299648 | tf_op jit(solution)/shard_map/reduce_sum | solution.py:36
  85.7 3.1 %maximum_convert_fusion = f32[4,8,32,3072]{3,2,1,0:T(8,128)S(1)} fusion(bf16[1,8,32,3072]{3,2,1,0:T(8,128)(2,1)} %bitcast.75, bf16[1,8,32,3072]{3,2,1,0:T(8,128)(2,1)} %bitcast.72, bf16[1,8,32,3072]{3,2,1,0:T(8,128)(2,1)S(1)} %bitcast.69, bf16[1,8,32,3072]{3,2,1,0:T(8,128)(2,1)S(1)} %copy-done.1), kind=kLoop, calls=%fused_computation.8 | loop fusion | flops 12582912 | bytes 18874368 | tf_op jit(solution)/shard_map/convert_element_type | solution.py:33
  88.8 5.1 %fusion.3 = bf16[1024,3072]{1,0:T(8,128)(2,1)} fusion(f32[4,8,32,3072]{3,2,1,0:T(8,128)S(1)} %maximum_convert_fusion, f32[3072]{0:T(1024)S(1)} %bitcast.77, f32[3072]{0:T(1024)S(1)} %bitcast.76, f32[1024]{0:T(1024)S(1)} %rsqrt.12, f32[1024]{0:T(1024)S(1)} %div.16), kind=kLoop, calls=%fused_computation.5 | loop fusion | flops 15728640 | bytes 18907136 | tf_op jit(solution)/shard_map/convert_element_type | solution.py:37
  93.9 12.5 %convolution_convert_fusion = bf16[1024,1152]{1,0:T(8,128)(2,1)S(1)} fusion(bf16[1024,3072]{1,0:T(8,128)(2,1)} %fusion.3, bf16[3072,1152]{0,1:T(8,128)(2,1)} %all-gather.2.cloned.1.call-done), kind=kOutput, calls=%fused_computation.9 | convolution fusion | flops 7248936960 | bytes 15728640 | tf_op jit(solution)/shard_map/dot_general | solution.py:152
  109.2 1.9 collective-permute-start.5
  111.2 12.6 %collective-permute-done.3 = bf16[256,1152]{1,0:T(8,128)(2,1)S(1)} collective-permute-done((bf16[256,1152]{1,0:T(8,128)(2,1)}, bf16[256,1152]{1,0:T(8,128)(2,1)S(1)}, u32[]{:S(2)}, u32[]{:S(2)}) %collective-permute-start.3) | collective-permute-done | bytes 589856 | tf_op jit(solution)/shard_map/ppermute | solution.py:158
  123.9 11.1 %collective-permute-done.5 = bf16[256,1152]{1,0:T(8,128)(2,1)S(1)} collective-permute-done((bf16[256,1152]{1,0:T(8,128)(2,1)S(1)}, bf16[256,1152]{1,0:T(8,128)(2,1)S(1)}, u32[]{:S(2)}, u32[]{:S(2)}) %collective-permute-start.5) | collective-permute-done | bytes 589856 | tf_op jit(solution)/shard_map/ppermute | solution.py:158
  137.4 2.4 reshape_reshape.21
  141.3 4.3 %collective-permute-start.6 = (bf16[8,32,3072]{2,1,0:T(8,128)(2,1)S(1)}, bf16[8,32,3072]{2,1,0:T(8,128)(2,1)S(1)}, u32[]{:S(2)}, u32[]{:S(2)}) collective-permute-start(bf16[8,32,3072]{2,1,0:T(8,128)(2,1)S(1)} %slice.48), channel_id=1, source_target_pairs={{0,32},{32,64},{64,96},{96,128},{128,160},{160,192},{192,224},{1,3... | collective-permute-start | bytes 4718600 | tf_op jit(solution)/shard_map/ppermute | solution.py:26
  145.6 3.4 %collective-permute-start.7 = (bf16[8,32,3072]{2,1,0:T(8,128)(2,1)S(1)}, bf16[8,32,3072]{2,1,0:T(8,128)(2,1)S(1)}, u32[]{:S(2)}, u32[]{:S(2)}) collective-permute-start(bf16[8,32,3072]{2,1,0:T(8,128)(2,1)S(1)} %slice.48), channel_id=1, source_target_pairs={{32,0},{64,32},{96,64},{128,96},{160,128},{192,160},{224,192},{33,... | collective-permute-start | bytes 4718600 | tf_op jit(solution)/shard_map/ppermute | solution.py:27
  149.0 30.8 %collective-permute-done.6 = bf16[8,32,3072]{2,1,0:T(8,128)(2,1)S(1)} collective-permute-done((bf16[8,32,3072]{2,1,0:T(8,128)(2,1)S(1)}, bf16[8,32,3072]{2,1,0:T(8,128)(2,1)S(1)}, u32[]{:S(2)}, u32[]{:S(2)}) %collective-permute-start.6) | collective-permute-done | bytes 1572896 | tf_op jit(solution)/shard_map/ppermute | solution.py:26
  179.9 31.1 %collective-permute-done.7 = bf16[8,32,3072]{2,1,0:T(8,128)(2,1)S(1)} collective-permute-done((bf16[8,32,3072]{2,1,0:T(8,128)(2,1)S(1)}, bf16[8,32,3072]{2,1,0:T(8,128)(2,1)S(1)}, u32[]{:S(2)}, u32[]{:S(2)}) %collective-permute-start.7) | collective-permute-done | bytes 1572896 | tf_op jit(solution)/shard_map/ppermute | solution.py:27
  213.8 4.7 %collective-permute-start.8 = (bf16[24,8,3072]{2,1,0:T(8,128)(2,1)}, bf16[24,8,3072]{2,1,0:T(8,128)(2,1)}, u32[]{:S(2)}, u32[]{:S(2)}) collective-permute-start(bf16[24,8,3072]{2,1,0:T(8,128)(2,1)} %get-tuple-element.5), channel_id=1, source_target_pairs={{0,8},{8,16},{16,24},{1,9},{9,17},{17,25},{2,10},{10,18},{18,26},{... | collective-permute-start | bytes 3538952 | tf_op jit(solution)/shard_map/ppermute | solution.py:26
  218.5 2.5 collective-permute-start.9
  223.1 2.1 copy_bitcast_fusion.1.q_ref
  225.2 6.7 %collective-permute-done.8 = bf16[24,8,3072]{2,1,0:T(8,128)(2,1)} collective-permute-done((bf16[24,8,3072]{2,1,0:T(8,128)(2,1)}, bf16[24,8,3072]{2,1,0:T(8,128)(2,1)}, u32[]{:S(2)}, u32[]{:S(2)}) %collective-permute-start.8) | collective-permute-done | bytes 1179680 | tf_op jit(solution)/shard_map/ppermute | solution.py:26
  231.9 4.4 %collective-permute-done.9 = bf16[24,8,3072]{2,1,0:T(8,128)(2,1)} collective-permute-done((bf16[24,8,3072]{2,1,0:T(8,128)(2,1)}, bf16[24,8,3072]{2,1,0:T(8,128)(2,1)}, u32[]{:S(2)}, u32[]{:S(2)}) %collective-permute-start.9) | collective-permute-done | bytes 1179680 | tf_op jit(solution)/shard_map/ppermute | solution.py:27
  236.3 3.3 %pad_maximum_fusion = bf16[24,48,3072]{2,1,0:T(8,128)(2,1)S(1)} fusion(bf16[24,8,3072]{2,1,0:T(8,128)(2,1)} %collective-permute-done.9, bf16[8,32,3072]{2,1,0:T(8,128)(2,1)} %copy-done.4, bf16[8,32,3072]{2,1,0:T(8,128)(2,1)S(1)} %slice.48, bf16[8,32,3072]{2,1,0:T(8,128)(2,1)S(1)} %collective-permute-done.6, bf16[24,8,3072]{2,1,0:T(8,128)(2,1)} %collective-permute-done.8), kind=kLoop, calls=%fused_computation.7 | loop fusion | flops 35389440 | bytes 14155776 | tf_op jit(solution)/shard_map/concatenate | solution.py:28
  239.6 3.7 %copy.11 = bf16[3,6,8,8,3072]{4,3,2,1,0:T(8,128)(2,1)} copy(bf16[3,6,8,8,3072]{4,3,1,2,0:T(8,128)(2,1)S(1)} %bitcast.62) | data formatting | bytes 14155776 | tf_op jit(solution)/shard_map/transpose | solution.py:45
  243.3 23.0 %shard_map.73 = bf16[4,64,1536]{2,1,0:T(8,128)(2,1)} custom-call(s32[36]{0:T(128)} %reshape_reshape.19.codes_ref, s32[4]{0:T(128)} %bitcast.78, s32[36]{0:T(128)} %gather_fusion, bf16[4,64,1536]{2,1,0:T(8,128)(2,1)} %copy_bitcast_fusion.1.q_ref, bf16[18,64,3072]{2,1,0:T(8,128)(2,1)} %bitcast.63), custom_call_target="tpu_custom_call" | custom-call | tf_op jit(solution)/shard_map/pallas_call | solution.py:129
  266.3 2.1 copy_bitcast_fusion
  (49 shorter events, 16.9 us)
Async XLA Ops:
  6.5 215.2 %copy-start = (s32[8,16]{1,0:T(8,128)S(1)}, s32[8,16]{1,0:T(8,128)}, u32[]{:S(2)}) copy-start(s32[8,16]{1,0:T(8,128)} %param.13) | copy-start | bytes 1540
  6.5 75.2 %copy-start.1 = (bf16[1,8,32,3072]{3,2,1,0:T(8,128)(2,1)S(1)}, bf16[1,8,32,3072]{3,2,1,0:T(8,128)(2,1)}, u32[]{:S(2)}) copy-start(bf16[1,8,32,3072]{3,2,1,0:T(8,128)(2,1)} %param.7) | copy-start | bytes 4718596
  6.5 87.4 %all-gather.2.cloned.1.call-start = ((), (), s32[]{:S(2)}) async-start(), calls=%async_computation | async-start | bytes 7962624 | tf_op jit(solution)/shard_map/all_gather | solution.py:148
  7.3 35.7 %collective-permute-start = (bf16[8,32,3072]{2,1,0:T(8,128)(2,1)}, bf16[8,32,3072]{2,1,0:T(8,128)(2,1)S(1)}, u32[]{:S(2)}, u32[]{:S(2)}) collective-permute-start(bf16[8,32,3072]{2,1,0:T(8,128)(2,1)} %bitcast.64), channel_id=1, source_target_pairs={{0,8},{8,16},{16,24},{24,0},{1,9},{9,17},{17,25},{25,1},{2,10},{10... | collective-permute-start | bytes 4718600 | tf_op jit(solution)/shard_map/ppermute | solution.py:145
  9.1 68.5 %collective-permute-start.1 = (bf16[8,32,3072]{2,1,0:T(8,128)(2,1)}, bf16[8,32,3072]{2,1,0:T(8,128)(2,1)S(1)}, u32[]{:S(2)}, u32[]{:S(2)}) collective-permute-start(bf16[8,32,3072]{2,1,0:T(8,128)(2,1)} %bitcast.65), channel_id=1, source_target_pairs={{0,16},{8,24},{16,0},{24,8},{1,17},{9,25},{17,1},{25,9},{2,18},{10... | collective-permute-start | bytes 4718600 | tf_op jit(solution)/shard_map/ppermute | solution.py:145
  9.4 69.0 %collective-permute-start.2 = (bf16[8,32,3072]{2,1,0:T(8,128)(2,1)}, bf16[8,32,3072]{2,1,0:T(8,128)(2,1)S(1)}, u32[]{:S(2)}, u32[]{:S(2)}) collective-permute-start(bf16[8,32,3072]{2,1,0:T(8,128)(2,1)} %bitcast.66), channel_id=1, source_target_pairs={{0,24},{8,0},{16,8},{24,16},{1,25},{9,1},{17,9},{25,17},{2,26},{10... | collective-permute-start | bytes 4718600 | tf_op jit(solution)/shard_map/ppermute | solution.py:145
  77.7 1.2 copy-start.2
  78.3 3.3 %copy-start.3 = (bf16[8,32,3072]{2,1,0:T(8,128)(2,1)}, bf16[8,32,3072]{2,1,0:T(8,128)(2,1)S(1)}, u32[]{:S(2)}) copy-start(bf16[8,32,3072]{2,1,0:T(8,128)(2,1)S(1)} %collective-permute-done.2) | copy-start | bytes 4718596
  85.7 3.1 %copy-start.5 = (f32[1,3072]{1,0:T(1,128)S(1)}, f32[1,3072]{1,0:T(1,128)}, u32[]{:S(2)}) copy-start(f32[1,3072]{1,0:T(1,128)} %param.8) | copy-start | bytes 36868
  107.6 16.1 %collective-permute-start.3 = (bf16[256,1152]{1,0:T(8,128)(2,1)}, bf16[256,1152]{1,0:T(8,128)(2,1)S(1)}, u32[]{:S(2)}, u32[]{:S(2)}) collective-permute-start(bf16[256,1152]{1,0:T(8,128)(2,1)} %get-tuple-element.9), channel_id=1, source_target_pairs={{0,24},{8,0},{16,8},{24,16},{1,25},{9,1},{17,9},{25,17},{2,26},{10... | collective-permute-start | bytes 1769480 | tf_op jit(solution)/shard_map/ppermute | solution.py:158
  108.0 15.8 %collective-permute-start.4 = (bf16[256,1152]{1,0:T(8,128)(2,1)}, bf16[256,1152]{1,0:T(8,128)(2,1)S(1)}, u32[]{:S(2)}, u32[]{:S(2)}) collective-permute-start(bf16[256,1152]{1,0:T(8,128)(2,1)} %get-tuple-element.8), channel_id=1, source_target_pairs={{0,16},{8,24},{16,0},{24,8},{1,17},{9,25},{17,1},{25,9},{2,18},{10... | collective-permute-start | bytes 1769480 | tf_op jit(solution)/shard_map/ppermute | solution.py:158
  109.2 25.7 %collective-permute-start.5 = (bf16[256,1152]{1,0:T(8,128)(2,1)S(1)}, bf16[256,1152]{1,0:T(8,128)(2,1)S(1)}, u32[]{:S(2)}, u32[]{:S(2)}) collective-permute-start(bf16[256,1152]{1,0:T(8,128)(2,1)S(1)} %get-tuple-element.7), channel_id=1, source_target_pairs={{0,8},{8,16},{16,24},{24,0},{1,9},{9,17},{17,25},{25,1},{2,10},{10... | collective-permute-start | bytes 1769480 | tf_op jit(solution)/shard_map/ppermute | solution.py:158
  139.8 81.2 %copy-start.6 = (s32[1,4,9]{2,1,0:T(4,128)S(1)}, s32[1,4,9]{2,1,0:T(4,128)}, u32[]{:S(2)}) copy-start(s32[1,4,9]{2,1,0:T(4,128)} %param.11) | copy-start | bytes 436
  141.3 38.5 %collective-permute-start.6 = (bf16[8,32,3072]{2,1,0:T(8,128)(2,1)S(1)}, bf16[8,32,3072]{2,1,0:T(8,128)(2,1)S(1)}, u32[]{:S(2)}, u32[]{:S(2)}) collective-permute-start(bf16[8,32,3072]{2,1,0:T(8,128)(2,1)S(1)} %slice.48), channel_id=1, source_target_pairs={{0,32},{32,64},{64,96},{96,128},{128,160},{160,192},{192,224},{1,3... | collective-permute-start | bytes 4718600 | tf_op jit(solution)/shard_map/ppermute | solution.py:26
  145.6 65.4 %collective-permute-start.7 = (bf16[8,32,3072]{2,1,0:T(8,128)(2,1)S(1)}, bf16[8,32,3072]{2,1,0:T(8,128)(2,1)S(1)}, u32[]{:S(2)}, u32[]{:S(2)}) collective-permute-start(bf16[8,32,3072]{2,1,0:T(8,128)(2,1)S(1)} %slice.48), channel_id=1, source_target_pairs={{32,0},{64,32},{96,64},{128,96},{160,128},{192,160},{224,192},{33,... | collective-permute-start | bytes 4718600 | tf_op jit(solution)/shard_map/ppermute | solution.py:27
  211.0 1.1 copy-start.4
  213.8 18.1 %collective-permute-start.8 = (bf16[24,8,3072]{2,1,0:T(8,128)(2,1)}, bf16[24,8,3072]{2,1,0:T(8,128)(2,1)}, u32[]{:S(2)}, u32[]{:S(2)}) collective-permute-start(bf16[24,8,3072]{2,1,0:T(8,128)(2,1)} %get-tuple-element.5), channel_id=1, source_target_pairs={{0,8},{8,16},{16,24},{1,9},{9,17},{17,25},{2,10},{10,18},{18,26},{... | collective-permute-start | bytes 3538952 | tf_op jit(solution)/shard_map/ppermute | solution.py:26
  218.5 17.8 %collective-permute-start.9 = (bf16[24,8,3072]{2,1,0:T(8,128)(2,1)}, bf16[24,8,3072]{2,1,0:T(8,128)(2,1)}, u32[]{:S(2)}, u32[]{:S(2)}) collective-permute-start(bf16[24,8,3072]{2,1,0:T(8,128)(2,1)} %get-tuple-element.6), channel_id=1, source_target_pairs={{8,0},{16,8},{24,16},{9,1},{17,9},{25,17},{10,2},{18,10},{26,18},{... | collective-permute-start | bytes 3538952 | tf_op jit(solution)/shard_map/ppermute | solution.py:27
Sparse Core Ops, SparseCore 0:
  9.1 84.3 all-gather.1

commit v5 on v4

--- a/solution.py
+++ b/solution.py
@@ -158,11 +158,32 @@
         lax.ppermute(partial[d], "gx", [(i, (i - d) % group) for i in range(group)])
         for d in range(1, group)
     ]
-    doubled = jnp.stack(returned + returned)
-    ordered = lax.dynamic_slice_in_dim(doubled, group - me, group, axis=0)
-    qkv = ordered.transpose(1, 0, 2).reshape(tile_rows * tile_cols, 3 * width)
-    qkv_grid = qkv.reshape(tile_rows, tile_cols, 3 * width)
-    extended = extended_2(qkv_grid[:, :, width:], (("gy", 0), ("gx", 1)), BLK)
+    rows_axis = lax.axis_size("gy")
+    block = partial.shape[-1]
+    senders = [g for g in range(group) if (g + 1) * block > width]
+
+    def neighbour_rows(step):
+        chunks = []
+        for d in range(group):
+            pairs = [
+                (r * group + g, (r + step) * group + (g - d) % group)
+                for r in range(rows_axis)
+                if 0 <= r + step < rows_axis
+                for g in senders
+            ]
+            chunks.append(lax.ppermute(partial[d], ("gy", "gx"), pairs))
+        return assemble(chunks)[:, :, width:]
+
+    def assemble(chunks):
+        doubled = jnp.stack(chunks + chunks)
+        ordered = lax.dynamic_slice_in_dim(doubled, group - me, group, axis=0)
+        return ordered.transpose(1, 0, 2).reshape(tile_rows, tile_cols, 3 * width)
+
+    above = neighbour_rows(1)
+    below = neighbour_rows(-1)
+    qkv_grid = assemble(returned)
+    extended = jnp.concatenate([above, qkv_grid[:, :, width:], below], axis=0)
+    extended = extended_2(extended, (("gx", 1),), BLK)
     block_rows = tile_rows // BLK
     block_cols = tile_cols // BLK
     queries = to_blocks(qkv_grid[:, :, :width])

time: 279 us -> 292 us (1.047)
  waiting for transfers between devices: 165 us -> 121 us
  local copies, waits for them, and re-layouts: 19.4 us -> 50.3 us
  starting transfers between devices: 20.7 us -> 48.1 us
    ppermute x2 -> x1, waiting for transfers between devices: 37.5 us -> 1.18 us  [extended_2(): before = lax.ppermute(last, axis, up)]
    ppermute x0 -> x8, starting transfers between devices: none -> 34.7 us  [neighbour_rows(): chunks.append(lax.ppermute(partial[d], ('gy', 'gx'), pairs))]
    ppermute x2 -> x1, waiting for transfers between devices: 35.5 us -> 7.77 us  [extended_2(): after = lax.ppermute(first, axis, down)]
    ppermute x0 -> x8, waiting for transfers between devices: none -> 26.6 us  [neighbour_rows(): chunks.append(lax.ppermute(partial[d], ('gy', 'gx'), pairs))]
    unnamed x21 -> x39, local copies, waits for them, and re-layouts: 2.11 us -> 11.6 us
    transpose x2 -> x5, local copies, waits for them, and re-layouts: 2.02 us -> 11.3 us  [assemble(): return ordered.transpose(1, 0, 2).reshape(tile_rows, tile_cols, 3 * width)]
    reshape x0 -> x3, local copies, waits for them, and re-layouts: none -> 9.08 us  [assemble(): return ordered.transpose(1, 0, 2).reshape(tile_rows, tile_cols, 3 * width)]
    ppermute x3, waiting for transfers between devices: 23.6 us -> 18.4 us  [body(): lax.ppermute(partial[d], 'gx', [(i, (i - d) % group) for i in range(group)])]
  transfers between devices with their start and end apart: 11 -> 17, of which waited for: 9 -> 12; matrix products, arithmetic and copies ran while one was open for 7% -> 10% of each run, Pallas kernels for 0% -> 0%
where the time goes in v5:
time: 292 us; the launch traced here: 290 us
  waiting for transfers between devices  121 us (41%)
  local copies, waits for them, and re-layouts  50.3 us (17%)
  starting transfers between devices  48.1 us (16%)
  Pallas kernels  22.7 us (8%)
  other arithmetic  21 us (7%)
  between operations  13.8 us (5%)
  matrix products  12.5 us (4%)
    ppermute x3, waiting for transfers between devices, body(): lax.ppermute(tile, 'gx', [(i, (i + d) % group) for i in range(group)])  66.1 us
    ppermute x8, starting transfers between devices, neighbour_rows(): chunks.append(lax.ppermute(partial[d], ('gy', 'gx'), pairs))  34.7 us
    ppermute x8, waiting for transfers between devices, neighbour_rows(): chunks.append(lax.ppermute(partial[d], ('gy', 'gx'), pairs))  26.6 us
    pallas_call x1, Pallas kernels, local_attention(): pl.pallas_call(functools.partial(attend_kernel, block_cols), grid_spec=gr...  22.7 us
    ppermute x3, waiting for transfers between devices, body(): lax.ppermute(partial[d], 'gx', [(i, (i - d) % group) for i in range(group)])  18.4 us
    dot_general x1, matrix products, body(): jnp.dot(strip.reshape(group * tile_rows * tile_cols, D), weight_block, pr...  12.5 us
    unnamed x39, local copies, waits for them, and re-layouts  11.6 us
    transpose x5, local copies, waits for them, and re-layouts, assemble(): return ordered.transpose(1, 0, 2).reshape(tile_rows, tile_cols, 3 * width)  11.3 us
  transfers between devices with their start and end apart: 17, of which 12 were waited for; matrix products, arithmetic and copies ran while one was open for 10% of the time, Pallas kernels for 0%

profile of v5, /device:TPU:25, one launch (start us, length us, event | category | flops | bytes accessed | tf_op | source)
XLA Modules:
  0.0 289.7 jit_solution(10807182673752368784)
XLA Ops:
  11.3 33.3 %collective-permute-done.2 = bf16[8,32,3072]{2,1,0:T(8,128)(2,1)S(1)} collective-permute-done((bf16[8,32,3072]{2,1,0:T(8,128)(2,1)}, bf16[8,32,3072]{2,1,0:T(8,128)(2,1)S(1)}, u32[]{:S(2)}, u32[]{:S(2)}) %collective-permute-start.2) | collective-permute-done | bytes 1572896 | tf_op jit(solution)/shard_map/ppermute | solution.py:145
  44.7 32.6 %collective-permute-done = bf16[8,32,3072]{2,1,0:T(8,128)(2,1)S(1)} collective-permute-done((bf16[8,32,3072]{2,1,0:T(8,128)(2,1)}, bf16[8,32,3072]{2,1,0:T(8,128)(2,1)S(1)}, u32[]{:S(2)}, u32[]{:S(2)}) %collective-permute-start) | collective-permute-done | bytes 1572896 | tf_op jit(solution)/shard_map/ppermute | solution.py:145
  77.4 3.2 %fusion.13 = f32[4,8,32]{2,1,0:T(8,128)S(1)} fusion(bf16[1,8,32,3072]{3,2,1,0:T(8,128)(2,1)S(1)} %bitcast.92, bf16[1,8,32,3072]{3,2,1,0:T(8,128)(2,1)S(1)} %bitcast.95, bf16[1,8,32,3072]{3,2,1,0:T(8,128)(2,1)S(1)} %bitcast.98, bf16[1,8,32,3072]{3,2,1,0:T(8,128)(2,1)} %param.7), kind=kLoop, calls=%fused_computation.65 | loop fusion | flops 15727616 | bytes 6295552 | tf_op jit(solution)/shard_map/reduce_sum | solution.py:34
  80.6 3.8 %multiply_reduce_fusion = f32[4,8,32]{2,1,0:T(8,128)S(1)} fusion(f32[4,8,32]{2,1,0:T(8,128)S(1)} %broadcast_multiply_fusion, bf16[1,8,32,3072]{3,2,1,0:T(8,128)(2,1)S(1)} %bitcast.93, bf16[1,8,32,3072]{3,2,1,0:T(8,128)(2,1)} %bitcast.96, bf16[1,8,32,3072]{3,2,1,0:T(8,128)(2,1)} %bitcast.99, bf16[1,8,32,3072]{3,2,1,0:T(8,128)(2,1)S(1)} %copy-done.2), kind=kLoop, calls=%fused_computation.6 | loop fusion | flops 22019072 | bytes 6299648 | tf_op jit(solution)/shard_map/reduce_sum | solution.py:36
  87.7 5.1 %fusion.3 = bf16[1024,3072]{1,0:T(8,128)(2,1)} fusion(f32[4,8,32,3072]{3,2,1,0:T(8,128)S(1)} %maximum_convert_fusion, f32[3072]{0:T(1024)S(1)} %bitcast.102, f32[3072]{0:T(1024)S(1)} %bitcast.101, f32[1024]{0:T(1024)S(1)} %rsqrt.12, f32[1024]{0:T(1024)S(1)} %div.16), kind=kLoop, calls=%fused_computation.5 | loop fusion | flops 15728640 | bytes 18907136 | tf_op jit(solution)/shard_map/convert_element_type | solution.py:37
  93.5 12.5 %convolution_convert_fusion = bf16[1024,1152]{1,0:T(8,128)(2,1)S(1)} fusion(bf16[1024,3072]{1,0:T(8,128)(2,1)} %fusion.3, bf16[3072,1152]{0,1:T(8,128)(2,1)} %all-gather.2.cloned.1.call-done), kind=kOutput, calls=%fused_computation.9 | convolution fusion | flops 7248936960 | bytes 15728640 | tf_op jit(solution)/shard_map/dot_general | solution.py:152
  110.1 4.7 %collective-permute-start.11 = (bf16[256,1152]{1,0:T(8,128)(2,1)}, bf16[256,1152]{1,0:T(8,128)(2,1)S(1)}, u32[]{:S(2)}, u32[]{:S(2)}) collective-permute-start(bf16[256,1152]{1,0:T(8,128)(2,1)} %get-tuple-element.10), channel_id=1, source_target_pairs={{40,0},{48,8},{56,16},{72,32},{80,40},{88,48},{104,64},{112,72},{1... | collective-permute-start | bytes 1769480 | tf_op jit(solution)/shard_map/ppermute | solution.py:174
  117.3 6.6 %collective-permute-done.3 = bf16[256,1152]{1,0:T(8,128)(2,1)S(1)} collective-permute-done((bf16[256,1152]{1,0:T(8,128)(2,1)}, bf16[256,1152]{1,0:T(8,128)(2,1)S(1)}, u32[]{:S(2)}, u32[]{:S(2)}) %collective-permute-start.3) | collective-permute-done | bytes 589856 | tf_op jit(solution)/shard_map/ppermute | solution.py:158
  129.8 11.8 %collective-permute-done.5 = bf16[256,1152]{1,0:T(8,128)(2,1)S(1)} collective-permute-done((bf16[256,1152]{1,0:T(8,128)(2,1)}, bf16[256,1152]{1,0:T(8,128)(2,1)S(1)}, u32[]{:S(2)}, u32[]{:S(2)}) %collective-permute-start.5) | collective-permute-done | bytes 589856 | tf_op jit(solution)/shard_map/ppermute | solution.py:158
  141.6 4.5 %collective-permute-start.6 = (bf16[256,1152]{1,0:T(8,128)(2,1)}, bf16[256,1152]{1,0:T(8,128)(2,1)S(1)}, u32[]{:S(2)}, u32[]{:S(2)}) collective-permute-start(bf16[256,1152]{1,0:T(8,128)(2,1)} %get-tuple-element.7), channel_id=1, source_target_pairs={{8,40},{16,48},{24,56},{40,72},{48,80},{56,88},{72,104},{80,112},{... | collective-permute-start | bytes 1769480 | tf_op jit(solution)/shard_map/ppermute | solution.py:174
  146.5 4.5 %collective-permute-done.10 = bf16[256,1152]{1,0:T(8,128)(2,1)S(1)} collective-permute-done((bf16[256,1152]{1,0:T(8,128)(2,1)}, bf16[256,1152]{1,0:T(8,128)(2,1)S(1)}, u32[]{:S(2)}, u32[]{:S(2)}) %collective-permute-start.10) | collective-permute-done | bytes 589856 | tf_op jit(solution)/shard_map/ppermute | solution.py:174
  150.9 4.8 %collective-permute-start.7 = (bf16[256,1152]{1,0:T(8,128)(2,1)}, bf16[256,1152]{1,0:T(8,128)(2,1)S(1)}, u32[]{:S(2)}, u32[]{:S(2)}) collective-permute-start(bf16[256,1152]{1,0:T(8,128)(2,1)} %get-tuple-element.10), channel_id=1, source_target_pairs={{8,32},{16,40},{24,48},{40,64},{48,72},{56,80},{72,96},{80,104},{8... | collective-permute-start | bytes 1769480 | tf_op jit(solution)/shard_map/ppermute | solution.py:174
  155.8 9.8 %collective-permute-start.8 = (bf16[256,1152]{1,0:T(8,128)(2,1)}, bf16[256,1152]{1,0:T(8,128)(2,1)}, u32[]{:S(2)}, u32[]{:S(2)}) collective-permute-start(bf16[256,1152]{1,0:T(8,128)(2,1)} %get-tuple-element.9), channel_id=1, source_target_pairs={{8,56},{16,32},{24,40},{40,88},{48,64},{56,72},{72,120},{80,96},{8... | collective-permute-start | bytes 1769480 | tf_op jit(solution)/shard_map/ppermute | solution.py:174
  169.9 8.4 %collective-permute-done.7 = bf16[256,1152]{1,0:T(8,128)(2,1)S(1)} collective-permute-done((bf16[256,1152]{1,0:T(8,128)(2,1)}, bf16[256,1152]{1,0:T(8,128)(2,1)S(1)}, u32[]{:S(2)}, u32[]{:S(2)}) %collective-permute-start.7) | collective-permute-done | bytes 589856 | tf_op jit(solution)/shard_map/ppermute | solution.py:174
  183.6 9.3 %collective-permute-done.8 = bf16[256,1152]{1,0:T(8,128)(2,1)} collective-permute-done((bf16[256,1152]{1,0:T(8,128)(2,1)}, bf16[256,1152]{1,0:T(8,128)(2,1)}, u32[]{:S(2)}, u32[]{:S(2)}) %collective-permute-start.8) | collective-permute-done | bytes 589856 | tf_op jit(solution)/shard_map/ppermute | solution.py:174
  194.9 4.4 %collective-permute-done.9 = bf16[256,1152]{1,0:T(8,128)(2,1)} collective-permute-done((bf16[256,1152]{1,0:T(8,128)(2,1)}, bf16[256,1152]{1,0:T(8,128)(2,1)}, u32[]{:S(2)}, u32[]{:S(2)}) %collective-permute-start.9) | collective-permute-done | bytes 589856 | tf_op jit(solution)/shard_map/ppermute | solution.py:174
  206.9 4.2 %dynamic-slice_bitcast_fusion = (bf16[256,4,1152]{2,0,1:T(8,128)(2,1)S(1)}, bf16[256,4,1152]{2,0,1:T(8,128)(2,1)}) fusion(bf16[8,256,1152]{2,1,0:T(8,128)(2,1)} %copy-done.6, s32[]{:T(128)S(6)} %select_n.27, bf16[8,256,1152]{2,1,0:T(8,128)(2,1)} %bitcast_dynamic-update-slice_fusion.9), kind=kLoop, calls=%fused_computation.10 | loop fusion | bytes 9437188 | tf_op jit(solution)/shard_map/transpose | solution.py:180
  218.6 3.3 %copy.11 = bf16[256,4,1152]{2,1,0:T(4,128)(2,1)} copy(bf16[256,4,1152]{2,0,1:T(8,128)(2,1)S(1)} %copy-done.5) | data formatting | bytes 4718592 | tf_op jit(solution)/shard_map/transpose | solution.py:180
  221.9 4.3 %reshape.76 = bf16[8,32,4608]{2,1,0:T(8,128)(2,1)} reshape(bf16[256,4,1152]{2,1,0:T(4,128)(2,1)} %copy.11) | data formatting | bytes 4718592 | tf_op jit(solution)/shard_map/reshape | solution.py:180
  232.4 5.5 %collective-permute-start.14 = (bf16[24,8,3072]{2,1,0:T(8,128)(2,1)}, bf16[24,8,3072]{2,1,0:T(8,128)(2,1)}, u32[]{:S(2)}, u32[]{:S(2)}) collective-permute-start(bf16[24,8,3072]{2,1,0:T(8,128)(2,1)} %get-tuple-element.5), channel_id=1, source_target_pairs={{0,8},{8,16},{16,24},{1,9},{9,17},{17,25},{2,10},{10,18},{18,26},{... | collective-permute-start | bytes 3538952 | tf_op jit(solution)/shard_map/ppermute | solution.py:26
  242.2 7.8 %collective-permute-done.15 = bf16[24,8,3072]{2,1,0:T(8,128)(2,1)} collective-permute-done((bf16[24,8,3072]{2,1,0:T(8,128)(2,1)}, bf16[24,8,3072]{2,1,0:T(8,128)(2,1)}, u32[]{:S(2)}, u32[]{:S(2)}) %collective-permute-start.15) | collective-permute-done | bytes 1179680 | tf_op jit(solution)/shard_map/ppermute | solution.py:27
  251.1 3.3 %pad_maximum_fusion = bf16[24,48,3072]{2,1,0:T(8,128)(2,1)S(1)} fusion(bf16[24,8,3072]{2,1,0:T(8,128)(2,1)} %collective-permute-done.15, bf16[8,32,3072]{2,1,0:T(8,128)(2,1)S(1)} %slice.66, bf16[8,32,3072]{2,1,0:T(8,128)(2,1)S(1)} %slice.65, bf16[8,32,3072]{2,1,0:T(8,128)(2,1)} %copy-done.1, bf16[24,8,3072]{2,1,0:T(8,128)(2,1)} %collective-permute-done.14), kind=kLoop, calls=%fused_computation.7 | loop fusion | flops 35389440 | bytes 14155776 | tf_op jit(solution)/shard_map/concatenate | solution.py:28
  254.4 3.7 %copy.13 = bf16[3,6,8,8,3072]{4,3,2,1,0:T(8,128)(2,1)} copy(bf16[3,6,8,8,3072]{4,3,1,2,0:T(8,128)(2,1)S(1)} %bitcast.87) | data formatting | bytes 14155776 | tf_op jit(solution)/shard_map/transpose | solution.py:45
  258.1 22.7 %shard_map.73 = bf16[4,64,1536]{2,1,0:T(8,128)(2,1)} custom-call(s32[36]{0:T(128)} %reshape_reshape.16.codes_ref, s32[4]{0:T(128)} %bitcast.103, s32[36]{0:T(128)} %gather_fusion, bf16[4,64,1536]{2,1,0:T(8,128)(2,1)} %copy_bitcast_fusion.1.q_ref, bf16[18,64,3072]{2,1,0:T(8,128)(2,1)} %bitcast.88), custom_call_target="tpu_custom_call" | custom-call | tf_op jit(solution)/shard_map/pallas_call | solution.py:129
  (88 shorter events, 62.1 us)
Async XLA Ops:
  6.5 232.2 %copy-start = (s32[8,16]{1,0:T(8,128)S(1)}, s32[8,16]{1,0:T(8,128)}, u32[]{:S(2)}) copy-start(s32[8,16]{1,0:T(8,128)} %param.13) | copy-start | bytes 1540
  6.5 74.1 %copy-start.2 = (bf16[1,8,32,3072]{3,2,1,0:T(8,128)(2,1)S(1)}, bf16[1,8,32,3072]{3,2,1,0:T(8,128)(2,1)}, u32[]{:S(2)}) copy-start(bf16[1,8,32,3072]{3,2,1,0:T(8,128)(2,1)} %param.7) | copy-start | bytes 4718596
  6.5 86.9 %all-gather.2.cloned.1.call-start = ((), (), s32[]{:S(2)}) async-start(), calls=%async_computation | async-start | bytes 7962624 | tf_op jit(solution)/shard_map/all_gather | solution.py:148
  7.3 37.3 %collective-permute-start.2 = (bf16[8,32,3072]{2,1,0:T(8,128)(2,1)}, bf16[8,32,3072]{2,1,0:T(8,128)(2,1)S(1)}, u32[]{:S(2)}, u32[]{:S(2)}) collective-permute-start(bf16[8,32,3072]{2,1,0:T(8,128)(2,1)} %bitcast.89), channel_id=1, source_target_pairs={{0,24},{8,0},{16,8},{24,16},{1,25},{9,1},{17,9},{25,17},{2,26},{10... | collective-permute-start | bytes 4718600 | tf_op jit(solution)/shard_map/ppermute | solution.py:145
  8.0 36.7 %collective-permute-start.1 = (bf16[8,32,3072]{2,1,0:T(8,128)(2,1)}, bf16[8,32,3072]{2,1,0:T(8,128)(2,1)S(1)}, u32[]{:S(2)}, u32[]{:S(2)}) collective-permute-start(bf16[8,32,3072]{2,1,0:T(8,128)(2,1)} %bitcast.90), channel_id=1, source_target_pairs={{0,16},{8,24},{16,0},{24,8},{1,17},{9,25},{17,1},{25,9},{2,18},{10... | collective-permute-start | bytes 4718600 | tf_op jit(solution)/shard_map/ppermute | solution.py:145
  9.2 68.1 %collective-permute-start = (bf16[8,32,3072]{2,1,0:T(8,128)(2,1)}, bf16[8,32,3072]{2,1,0:T(8,128)(2,1)S(1)}, u32[]{:S(2)}, u32[]{:S(2)}) collective-permute-start(bf16[8,32,3072]{2,1,0:T(8,128)(2,1)} %bitcast.91), channel_id=1, source_target_pairs={{0,8},{8,16},{16,24},{24,0},{1,9},{9,17},{17,25},{25,1},{2,10},{10... | collective-permute-start | bytes 4718600 | tf_op jit(solution)/shard_map/ppermute | solution.py:145
  44.7 32.6 %copy-start.3 = (bf16[8,32,3072]{2,1,0:T(8,128)(2,1)}, bf16[8,32,3072]{2,1,0:T(8,128)(2,1)S(1)}, u32[]{:S(2)}) copy-start(bf16[8,32,3072]{2,1,0:T(8,128)(2,1)S(1)} %collective-permute-done.1) | copy-start | bytes 4718596
  77.4 3.2 %copy-start.4 = (bf16[8,32,3072]{2,1,0:T(8,128)(2,1)}, bf16[8,32,3072]{2,1,0:T(8,128)(2,1)S(1)}, u32[]{:S(2)}) copy-start(bf16[8,32,3072]{2,1,0:T(8,128)(2,1)S(1)} %collective-permute-done) | copy-start | bytes 4718596
  107.4 16.5 %collective-permute-start.3 = (bf16[256,1152]{1,0:T(8,128)(2,1)}, bf16[256,1152]{1,0:T(8,128)(2,1)S(1)}, u32[]{:S(2)}, u32[]{:S(2)}) collective-permute-start(bf16[256,1152]{1,0:T(8,128)(2,1)} %get-tuple-element.10), channel_id=1, source_target_pairs={{0,24},{8,0},{16,8},{24,16},{1,25},{9,1},{17,9},{25,17},{2,26},{10... | collective-permute-start | bytes 1769480 | tf_op jit(solution)/shard_map/ppermute | solution.py:158
  108.9 18.2 %collective-permute-start.4 = (bf16[256,1152]{1,0:T(8,128)(2,1)}, bf16[256,1152]{1,0:T(8,128)(2,1)S(1)}, u32[]{:S(2)}, u32[]{:S(2)}) collective-permute-start(bf16[256,1152]{1,0:T(8,128)(2,1)} %get-tuple-element.9), channel_id=1, source_target_pairs={{0,16},{8,24},{16,0},{24,8},{1,17},{9,25},{17,1},{25,9},{2,18},{10... | collective-permute-start | bytes 1769480 | tf_op jit(solution)/shard_map/ppermute | solution.py:158
  110.1 45.7 %collective-permute-start.11 = (bf16[256,1152]{1,0:T(8,128)(2,1)}, bf16[256,1152]{1,0:T(8,128)(2,1)S(1)}, u32[]{:S(2)}, u32[]{:S(2)}) collective-permute-start(bf16[256,1152]{1,0:T(8,128)(2,1)} %get-tuple-element.10), channel_id=1, source_target_pairs={{40,0},{48,8},{56,16},{72,32},{80,40},{88,48},{104,64},{112,72},{1... | collective-permute-start | bytes 1769480 | tf_op jit(solution)/shard_map/ppermute | solution.py:174
  114.8 50.8 %collective-permute-start.12 = (bf16[256,1152]{1,0:T(8,128)(2,1)}, bf16[256,1152]{1,0:T(8,128)(2,1)S(1)}, u32[]{:S(2)}, u32[]{:S(2)}) collective-permute-start(bf16[256,1152]{1,0:T(8,128)(2,1)} %get-tuple-element.9), channel_id=1, source_target_pairs={{40,24},{48,0},{56,8},{72,56},{80,32},{88,40},{104,88},{112,64},{1... | collective-permute-start | bytes 1769480 | tf_op jit(solution)/shard_map/ppermute | solution.py:174
  117.2 24.4 %collective-permute-start.5 = (bf16[256,1152]{1,0:T(8,128)(2,1)}, bf16[256,1152]{1,0:T(8,128)(2,1)S(1)}, u32[]{:S(2)}, u32[]{:S(2)}) collective-permute-start(bf16[256,1152]{1,0:T(8,128)(2,1)} %get-tuple-element.8), channel_id=1, source_target_pairs={{0,8},{8,16},{16,24},{24,0},{1,9},{9,17},{17,25},{25,1},{2,10},{10... | collective-permute-start | bytes 1769480 | tf_op jit(solution)/shard_map/ppermute | solution.py:158
  123.9 44.7 %collective-permute-start.13 = (bf16[256,1152]{1,0:T(8,128)(2,1)}, bf16[256,1152]{1,0:T(8,128)(2,1)S(1)}, u32[]{:S(2)}, u32[]{:S(2)}) collective-permute-start(bf16[256,1152]{1,0:T(8,128)(2,1)} %get-tuple-element.8), channel_id=1, source_target_pairs={{40,16},{48,24},{56,0},{72,48},{80,56},{88,32},{104,80},{112,88},{... | collective-permute-start | bytes 1769480 | tf_op jit(solution)/shard_map/ppermute | solution.py:174
  127.1 23.9 %collective-permute-start.10 = (bf16[256,1152]{1,0:T(8,128)(2,1)}, bf16[256,1152]{1,0:T(8,128)(2,1)S(1)}, u32[]{:S(2)}, u32[]{:S(2)}) collective-permute-start(bf16[256,1152]{1,0:T(8,128)(2,1)} %get-tuple-element.7), channel_id=1, source_target_pairs={{40,8},{48,16},{56,24},{72,40},{80,48},{88,56},{104,72},{112,80},{... | collective-permute-start | bytes 1769480 | tf_op jit(solution)/shard_map/ppermute | solution.py:174
  141.6 27.3 %collective-permute-start.6 = (bf16[256,1152]{1,0:T(8,128)(2,1)}, bf16[256,1152]{1,0:T(8,128)(2,1)S(1)}, u32[]{:S(2)}, u32[]{:S(2)}) collective-permute-start(bf16[256,1152]{1,0:T(8,128)(2,1)} %get-tuple-element.7), channel_id=1, source_target_pairs={{8,40},{16,48},{24,56},{40,72},{48,80},{56,88},{72,104},{80,112},{... | collective-permute-start | bytes 1769480 | tf_op jit(solution)/shard_map/ppermute | solution.py:174
  150.9 27.4 %collective-permute-start.7 = (bf16[256,1152]{1,0:T(8,128)(2,1)}, bf16[256,1152]{1,0:T(8,128)(2,1)S(1)}, u32[]{:S(2)}, u32[]{:S(2)}) collective-permute-start(bf16[256,1152]{1,0:T(8,128)(2,1)} %get-tuple-element.10), channel_id=1, source_target_pairs={{8,32},{16,40},{24,48},{40,64},{48,72},{56,80},{72,96},{80,104},{8... | collective-permute-start | bytes 1769480 | tf_op jit(solution)/shard_map/ppermute | solution.py:174
  155.8 37.2 %collective-permute-start.8 = (bf16[256,1152]{1,0:T(8,128)(2,1)}, bf16[256,1152]{1,0:T(8,128)(2,1)}, u32[]{:S(2)}, u32[]{:S(2)}) collective-permute-start(bf16[256,1152]{1,0:T(8,128)(2,1)} %get-tuple-element.9), channel_id=1, source_target_pairs={{8,56},{16,32},{24,40},{40,88},{48,64},{56,72},{72,120},{80,96},{8... | collective-permute-start | bytes 1769480 | tf_op jit(solution)/shard_map/ppermute | solution.py:174
  165.7 33.6 %collective-permute-start.9 = (bf16[256,1152]{1,0:T(8,128)(2,1)}, bf16[256,1152]{1,0:T(8,128)(2,1)}, u32[]{:S(2)}, u32[]{:S(2)}) collective-permute-start(bf16[256,1152]{1,0:T(8,128)(2,1)} %get-tuple-element.8), channel_id=1, source_target_pairs={{8,48},{16,56},{24,32},{40,80},{48,88},{56,64},{72,112},{80,120},{... | collective-permute-start | bytes 1769480 | tf_op jit(solution)/shard_map/ppermute | solution.py:174
  169.0 9.4 %copy-start.6 = (bf16[8,256,1152]{2,1,0:T(8,128)(2,1)}, bf16[8,256,1152]{2,1,0:T(8,128)(2,1)S(1)}, u32[]{:S(2)}) copy-start(bf16[8,256,1152]{2,1,0:T(8,128)(2,1)S(1)} %bitcast_dynamic-update-slice_fusion.1) | copy-start | bytes 14155780
  215.3 3.3 %copy-start.5 = (bf16[256,4,1152]{2,0,1:T(8,128)(2,1)S(1)}, bf16[256,4,1152]{2,0,1:T(8,128)(2,1)}, u32[]{:S(2)}) copy-start(bf16[256,4,1152]{2,0,1:T(8,128)(2,1)} %get-tuple-element.14) | copy-start | bytes 7077892
  226.1 11.8 %copy-start.8 = (s32[1,4,9]{2,1,0:T(4,128)S(1)}, s32[1,4,9]{2,1,0:T(4,128)}, u32[]{:S(2)}) copy-start(s32[1,4,9]{2,1,0:T(4,128)} %param.11) | copy-start | bytes 436
  230.5 19.4 %collective-permute-start.15 = (bf16[24,8,3072]{2,1,0:T(8,128)(2,1)}, bf16[24,8,3072]{2,1,0:T(8,128)(2,1)}, u32[]{:S(2)}, u32[]{:S(2)}) collective-permute-start(bf16[24,8,3072]{2,1,0:T(8,128)(2,1)} %get-tuple-element.6), channel_id=1, source_target_pairs={{8,0},{16,8},{24,16},{9,1},{17,9},{25,17},{10,2},{18,10},{26,18},{... | collective-permute-start | bytes 3538952 | tf_op jit(solution)/shard_map/ppermute | solution.py:27
  232.4 18.7 %collective-permute-start.14 = (bf16[24,8,3072]{2,1,0:T(8,128)(2,1)}, bf16[24,8,3072]{2,1,0:T(8,128)(2,1)}, u32[]{:S(2)}, u32[]{:S(2)}) collective-permute-start(bf16[24,8,3072]{2,1,0:T(8,128)(2,1)} %get-tuple-element.5), channel_id=1, source_target_pairs={{0,8},{8,16},{16,24},{1,9},{9,17},{17,25},{2,10},{10,18},{18,26},{... | collective-permute-start | bytes 3538952 | tf_op jit(solution)/shard_map/ppermute | solution.py:26
  (2 other events, 4.4 us)
Sparse Core Ops, SparseCore 0:
  9.1 84.3 all-gather.1
